TPU v7x, 32 devices: a whole 2x2x4 slice. The times are simulated.
32 devices in a mesh: seq: 4 (over x, core), dp: 8 (over z, y).
Axes of the slice: x: 2, y: 2, z: 4, core: 2. Of those that a mesh axis runs over, the one named last changes fastest.
Arguments:
- tokens: bfloat16 [8, 2048, 768], P('dp', 'seq'), may hold values from -6 to 6
- prior_logits: float32 [8, 2048, 12], P('dp', 'seq'), may hold values from -6 to 6
- routes: int32 [8, 2048, 2], P('dp', 'seq'), may hold values from 0 to 11, all different within a row; in each aligned block of 2048 rows (0 to 2047, 2048 to 4095, ..., all dimensions but the last counted through in order) at most 512 rows name the same one
- cotangent: bfloat16 [8, 2048, 768], P('dp', 'seq'), may hold values from -6 to 6
- masters: float32 [416, 768, 128], P(('seq', 'dp'))
- owner: int32 [4, 102], P('seq'), may hold values from 0 to 103, as said below
- stat_left: float32 [416, 768, 768], P(('seq', 'dp'))
- stat_right: float32 [416, 128, 128], P(('seq', 'dp'))
- root_left: float32 [416, 768, 768], P(('seq', 'dp'))
- root_right: float32 [416, 128, 128], P(('seq', 'dp'))
- gain_attn: float32 [768], replicated, may hold values from 0.5 to 1.5
- gain_moe: float32 [768], replicated, may hold values from 0.5 to 1.5
- router: float32 [768, 12], replicated, may hold values from -0.21875 to 0.21875
- router_prior: float32 [12, 12], replicated, may hold values from -1.75 to 1.75
- const_mix: float32 [2, 768, 2], replicated, may hold values from -0.21875 to 0.21875
- const_value: float32 [2, 768], replicated, may hold values from -6 to 6
- adam_first: float32 [15504], replicated
- adam_second: float32 [15504], replicated
Outputs:
- block_out: bfloat16 [8, 2048, 768], P('dp', 'seq')
- input_grad: float32 [8, 2048, 768], P('dp', 'seq')
- prior_grad: float32 [8, 2048, 12], P('dp', 'seq')
- block_grads: float32 [416, 768, 128], P(('seq', 'dp'))
- new_masters: float32 [416, 768, 128], P(('seq', 'dp'))
- new_left: float32 [416, 768, 768], P(('seq', 'dp'))
- new_right: float32 [416, 128, 128], P(('seq', 'dp'))
- small_grads: float32 [15504], replicated
- new_small: float32 [15504], replicated
- new_first: float32 [15504], replicated
- new_second: float32 [15504], replicated
Inputs may be any that keep to these rules, and one draw needn't show every extreme that they name: In each sequence no route is named by more than 512 choices; a token's two routes differ. `owner`: the 102 entries of a row are distinct slots.
All inputs are finite; a program needn't handle non-finite values.
Results may differ from a plain program's by a relative error of at most 0.02.
Values may be sent and summed in bfloat16 or wider, within the bound.
No kernel may reach another device: no remote copies, remote signals or barrier semaphores. Data moves between devices by JAX's collectives and lax.ppermute only.
A program may use at most 320 MiB of HBM per device.

v0:
```python
from functools import partial

import jax
import jax.numpy as jnp
from jax import lax
from jax.sharding import PartitionSpec as P

D = 768
HEADS = 12
HEAD = 64
EXPERTS = 8
BW = 128
STEP = 4


norm_eps = 1e-06
rope_base = 10000.0
stat_decay = 0.5
shampoo_rate = 0.1
adam_rate = 0.01
first_decay = 0.9
second_decay = 0.999
adam_eps = 1e-08


def rms_scale(values, gain):
    return values * lax.rsqrt(jnp.mean(values * values, axis=-1, keepdims=True) + norm_eps) * gain


def rotate(values, positions):
    half_dim = values.shape[-1] // 2
    freq = rope_base ** (-(jnp.arange(half_dim, dtype=jnp.float32) * 2.0 / values.shape[-1]))
    angles = positions[:, None].astype(jnp.float32) * freq[None, :]
    cosine = jnp.cos(angles)[:, None, :]
    sine = jnp.sin(angles)[:, None, :]
    first_half = values[..., :half_dim]
    second_half = values[..., half_dim:]
    return jnp.concatenate(
        [first_half * cosine - second_half * sine, second_half * cosine + first_half * sine],
        axis=-1,
    )


def group_slots(route_flat, capacity, expert_count):
    pair_total = route_flat.shape[0]
    order = jnp.argsort(route_flat * pair_total + jnp.arange(pair_total, dtype=jnp.int32))
    counts = jnp.sum(
        (route_flat[None, :] == jnp.arange(expert_count, dtype=jnp.int32)[:, None]).astype(
            jnp.int32
        ),
        axis=1,
    )
    starts = jnp.cumsum(counts) - counts
    padded = jnp.concatenate([order, jnp.zeros((capacity,), jnp.int32)])
    pair_ids = jax.vmap(lambda begin: lax.dynamic_slice_in_dim(padded, begin, capacity))(starts)
    valid = jnp.arange(capacity, dtype=jnp.int32)[None, :] < counts[:, None]
    return (pair_ids, valid)


def local_experts(hidden, picked, route_rows, const_mix, const_value):
    highest = lax.Precision.HIGHEST
    copy_weight = jnp.sum(picked * (route_rows == EXPERTS + 1), axis=1)
    mixing = jax.nn.softmax(
        jnp.einsum("td,cdm->ctm", hidden, const_mix, precision=highest), axis=-1
    )
    result = copy_weight[:, None] * hidden
    for const_id in range(2):
        weight = jnp.sum(picked * (route_rows == EXPERTS + 2 + const_id), axis=1)
        result = result + weight[:, None] * (
            mixing[const_id][:, 0:1] * hidden
            + mixing[const_id][:, 1:2] * const_value[const_id][None, :]
        )
    return result


def local_part(route_rows, hidden, prior_rows, router, router_prior, const_mix, const_value):
    highest = lax.Precision.HIGHEST
    logits = jnp.dot(hidden, router, precision=highest) + jnp.dot(
        prior_rows, router_prior, precision=highest
    )
    chosen = jnp.take_along_axis(logits, route_rows, axis=1)
    picked = jax.nn.softmax(chosen, axis=-1)
    return (local_experts(hidden, picked, route_rows, const_mix, const_value), picked)


def arrange_experts(pieces):
    nj_count = pieces.shape[0] // (3 * EXPERTS)
    shaped = pieces.reshape(EXPERTS, 3, nj_count, D, BW)
    return shaped.transpose(0, 1, 3, 2, 4).reshape(EXPERTS, 3, D, nj_count * BW)


def add_rows(total, piece, offset):
    current = lax.dynamic_slice_in_dim(total, offset, piece.shape[0], 0)
    return lax.dynamic_update_slice_in_dim(total, current + piece, offset, 0)


def over_blocks(carry, keys_in, values_in, block_len, step_fn):
    count = keys_in.shape[0]
    steps_count = count // block_len

    def scan_step(inner, block_in):
        key_block, value_block, offset = block_in
        return (step_fn(inner, key_block, value_block, offset), None)

    offsets = jnp.arange(steps_count, dtype=jnp.int32) * block_len
    carry, _ = lax.scan(
        scan_step,
        carry,
        (
            keys_in.reshape(steps_count, block_len, -1),
            values_in.reshape(steps_count, block_len, -1),
            offsets,
        ),
    )
    return carry


def shampoo_update(masters, grads, stat_left, stat_right, root_left, root_right):
    highest = lax.Precision.HIGHEST
    new_left = stat_decay * stat_left + (1.0 - stat_decay) * jnp.einsum(
        "sik,sjk->sij", grads, grads, precision=highest
    )
    new_right = stat_decay * stat_right + (1.0 - stat_decay) * jnp.einsum(
        "ski,skj->sij", grads, grads, precision=highest
    )
    update = jnp.einsum("sij,sjk->sik", root_left, grads, precision=highest)
    update = jnp.einsum("sik,skl->sil", update, root_right, precision=highest)
    return (masters - shampoo_rate * update, new_left, new_right)


def pack_small(gain_attn, gain_moe, router, router_prior, const_mix, const_value):
    return jnp.concatenate(
        [
            gain_attn,
            gain_moe,
            router.reshape(-1),
            router_prior.reshape(-1),
            const_mix.reshape(-1),
            const_value.reshape(-1),
        ]
    )


def adam_update(params_flat, grads_flat, first, second):
    new_first = first_decay * first + (1.0 - first_decay) * grads_flat
    new_second = second_decay * second + (1.0 - second_decay) * grads_flat * grads_flat
    corrected_first = new_first / (1.0 - first_decay**STEP)
    corrected_second = new_second / (1.0 - second_decay**STEP)
    return (
        params_flat - adam_rate * corrected_first / (jnp.sqrt(corrected_second) + adam_eps),
        new_first,
        new_second,
    )


def body(
    tokens,
    prior_logits,
    routes,
    cotangent,
    masters,
    owner,
    stat_left,
    stat_right,
    root_left,
    root_right,
    gain_attn,
    gain_moe,
    router,
    router_prior,
    const_mix,
    const_value,
    adam_first,
    adam_second,
):
    highest = lax.Precision.HIGHEST
    f32 = jnp.float32
    bf16 = jnp.bfloat16
    seq_count = lax.axis_size("seq")
    dp_count = lax.axis_size("dp")
    seq_rank = lax.axis_index("seq")
    tok_rows = tokens.shape[1]
    group_rows = tok_rows * seq_count
    capacity = group_rows // 4
    row_slots = masters.shape[0] * dp_count
    attn_row = 4 * D // (BW * seq_count)
    score_scale = HEAD ** (-0.5)
    positions = seq_rank * tok_rows + jnp.arange(tok_rows, dtype=jnp.int32)
    last_query = seq_rank * tok_rows + tok_rows - 1
    row_pieces = lax.all_to_all(masters.astype(bf16), "dp", split_axis=1, concat_axis=0, tiled=True)
    choose = owner[0][:, None] == jnp.arange(row_slots, dtype=jnp.int32)[None, :]
    own_blocks = jnp.einsum(
        "bi,irc->brc", choose.astype(bf16), row_pieces, preferred_element_type=f32
    ).astype(bf16)
    shard_rows = own_blocks.shape[1]
    attn_pieces = lax.all_gather(own_blocks[:attn_row], ("seq", "dp"), axis=0, tiled=True)
    attn_full = (
        attn_pieces.reshape(seq_count, dp_count, attn_row, shard_rows, BW)
        .transpose(1, 3, 0, 2, 4)
        .reshape(D, 4 * D)
    )
    weight_qkv = attn_full[:, : 3 * D]
    weight_out = attn_full[:, 3 * D :]
    expert_w = arrange_experts(lax.all_gather(own_blocks[attn_row:], "dp", axis=1, tiled=True))
    x_rows = tokens[0].astype(f32)
    normed = rms_scale(x_rows, gain_attn)
    normed_b = normed.astype(bf16)
    projected = jnp.dot(normed_b, weight_qkv, preferred_element_type=f32)
    queries = rotate(projected[:, :D].reshape(tok_rows, HEADS, HEAD), positions).astype(bf16)
    keys_b = (
        rotate(projected[:, D : 2 * D].reshape(tok_rows, HEADS, HEAD), positions)
        .astype(bf16)
        .reshape(tok_rows, D)
    )
    values_b = projected[:, 2 * D :].astype(bf16)

    def forward_block(carry, key_block, value_block, offset):

        def forward_visit(inner):
            row_max, row_sum, accum = inner
            count = key_block.shape[0]
            key_heads = key_block.reshape(count, HEADS, HEAD)
            scores = (
                jnp.einsum("qhd,khd->hqk", queries, key_heads, preferred_element_type=f32)
                * score_scale
            )
            allowed = (offset + jnp.arange(count, dtype=jnp.int32))[None, :] <= positions[:, None]
            scores = jnp.where(allowed[None], scores, -1e30)
            new_max = jnp.maximum(row_max, jnp.max(scores, axis=-1))
            factor = jnp.exp(row_max - new_max)
            weights = jnp.where(allowed[None], jnp.exp(scores - new_max[..., None]), 0.0)
            row_sum = row_sum * factor + jnp.sum(weights, axis=-1)
            accum = accum * factor[..., None] + jnp.einsum(
                "hqk,khd->hqd",
                weights.astype(bf16),
                value_block.reshape(count, HEADS, HEAD),
                preferred_element_type=f32,
            )
            return (new_max, row_sum, accum)

        return lax.cond(offset <= last_query, forward_visit, lambda inner: inner, carry)

    fold_init = (
        jnp.full((HEADS, tok_rows), -1e30, f32),
        jnp.zeros((HEADS, tok_rows), f32),
        jnp.zeros((HEADS, tok_rows, HEAD), f32),
    )
    piece = (
        lax.all_gather(keys_b, "seq", axis=0, tiled=True),
        lax.all_gather(values_b, "seq", axis=0, tiled=True),
    )
    row_max, row_sum, accum = over_blocks(fold_init, piece[0], piece[1], tok_rows, forward_block)
    context = accum / row_sum[..., None]
    log_total = row_max + jnp.log(row_sum)
    context_b = context.transpose(1, 0, 2).reshape(tok_rows, D).astype(bf16)
    mid_rows = x_rows + jnp.dot(context_b, weight_out, preferred_element_type=f32)
    route_rows = routes[0]
    hidden = rms_scale(mid_rows, gain_moe)
    hidden_b = hidden.astype(bf16)
    (local_out, picked), local_back = jax.vjp(
        partial(local_part, route_rows),
        hidden,
        prior_logits[0],
        router,
        router_prior,
        const_mix,
        const_value,
    )
    group_in, group_codes, group_gates = (
        lax.all_gather(hidden_b, "seq", axis=0, tiled=True),
        lax.all_gather(route_rows.astype(bf16), "seq", axis=0, tiled=True),
        lax.all_gather(picked.astype(bf16), "seq", axis=0, tiled=True),
    )
    pair_ids, valid = group_slots(group_codes.reshape(-1).astype(jnp.int32), capacity, EXPERTS)
    token_ids = pair_ids // 2
    slot_gates = jnp.where(valid, group_gates.reshape(-1)[pair_ids].astype(f32), 0.0)
    expert_in = group_in[token_ids]
    gate_act = jnp.einsum("ecd,edf->ecf", expert_in, expert_w[:, 0], preferred_element_type=f32)
    up_act = jnp.einsum("ecd,edf->ecf", expert_in, expert_w[:, 1], preferred_element_type=f32)
    act_b = (jax.nn.silu(gate_act) * up_act).astype(bf16)
    expert_out = jnp.einsum("ecf,edf->ecd", act_b, expert_w[:, 2], preferred_element_type=f32)
    partial_out = (
        jnp.zeros((group_rows, D), f32)
        .at[token_ids.reshape(-1)]
        .add((expert_out * slot_gates[..., None]).reshape(-1, D))
    )
    moe_rows = lax.psum_scatter(
        partial_out.astype(jnp.bfloat16), "seq", scatter_dimension=0, tiled=True
    ).astype(jnp.float32)
    block_rows = mid_rows + moe_rows + local_out
    grad_b = cotangent[0]
    grad_rows = grad_b.astype(f32)
    group_grad = lax.all_gather(grad_b, "seq", axis=0, tiled=True)
    back_w = arrange_experts(lax.all_gather(own_blocks[attn_row:], "dp", axis=1, tiled=True))
    slot_grad = group_grad[token_ids].astype(f32)
    out_grad_b = (slot_grad * slot_gates[..., None]).astype(bf16)
    gate_grad_slots = jnp.where(valid, jnp.sum(slot_grad * expert_out, axis=-1), 0.0)
    act_grad = jnp.einsum("ecd,edf->ecf", out_grad_b, back_w[:, 2], preferred_element_type=f32)
    sigmoid_gate = jax.nn.sigmoid(gate_act)
    gate_grad_b = (
        act_grad * up_act * sigmoid_gate * (1.0 + gate_act * (1.0 - sigmoid_gate))
    ).astype(bf16)
    up_grad_b = (act_grad * gate_act * sigmoid_gate).astype(bf16)
    down_w_grad = jnp.einsum("ecf,ecd->edf", act_b, out_grad_b, preferred_element_type=f32)
    gate_w_grad = jnp.einsum("ecd,ecf->edf", expert_in, gate_grad_b, preferred_element_type=f32)
    up_w_grad = jnp.einsum("ecd,ecf->edf", expert_in, up_grad_b, preferred_element_type=f32)
    in_grad = jnp.einsum(
        "ecf,edf->ecd", gate_grad_b, back_w[:, 0], preferred_element_type=f32
    ) + jnp.einsum("ecf,edf->ecd", up_grad_b, back_w[:, 1], preferred_element_type=f32)
    token_grad = (
        jnp.zeros((group_rows, D), f32).at[token_ids.reshape(-1)].add(in_grad.reshape(-1, D))
    )
    pair_grad = (
        jnp.zeros((2 * group_rows,), f32)
        .at[pair_ids.reshape(-1)]
        .add(gate_grad_slots.reshape(-1))
        .reshape(group_rows, 2)
    )
    moe_grad, picked_grad = (
        lax.psum_scatter(
            token_grad.astype(jnp.bfloat16), "seq", scatter_dimension=0, tiled=True
        ).astype(jnp.float32),
        lax.psum_scatter(
            pair_grad.astype(jnp.bfloat16), "seq", scatter_dimension=0, tiled=True
        ).astype(jnp.float32),
    )
    hidden_local, prior_grad, router_grad, router_prior_grad, mix_grad, value_grad_small = (
        local_back((grad_rows, picked_grad))
    )
    hidden_grad = hidden_local + moe_grad
    _, second_norm_back = jax.vjp(rms_scale, mid_rows, gain_moe)
    mid_norm_grad, gain_moe_grad = second_norm_back(hidden_grad)
    mid_grad = grad_rows + mid_norm_grad
    attn_grad_b = mid_grad.astype(bf16)
    out_w_grad = jnp.dot(context_b.T, attn_grad_b, preferred_element_type=f32)
    context_grad_b = jnp.dot(attn_grad_b, weight_out.T, preferred_element_type=f32).astype(bf16)
    context_grad_heads = context_grad_b.reshape(tok_rows, HEADS, HEAD)
    delta = jnp.einsum("qhd,hqd->hq", context_grad_heads.astype(f32), context)

    def make_backward():

        def backward_block(carry, key_block, value_block, offset):

            def backward_visit(inner):
                query_grad = inner[0]
                count = key_block.shape[0]
                key_heads = key_block.reshape(count, HEADS, HEAD)
                value_heads = value_block.reshape(count, HEADS, HEAD)
                scores = (
                    jnp.einsum("qhd,khd->hqk", queries, key_heads, preferred_element_type=f32)
                    * score_scale
                )
                allowed = (offset + jnp.arange(count, dtype=jnp.int32))[None, :] <= positions[
                    :, None
                ]
                probs = jnp.where(allowed[None], jnp.exp(scores - log_total[..., None]), 0.0)
                prob_grad = jnp.einsum(
                    "qhd,khd->hqk", context_grad_heads, value_heads, preferred_element_type=f32
                )
                score_grad_b = (probs * (prob_grad - delta[..., None])).astype(bf16)
                query_grad = (
                    query_grad
                    + jnp.einsum(
                        "hqk,khd->qhd", score_grad_b, key_heads, preferred_element_type=f32
                    )
                    * score_scale
                )
                value_part = jnp.einsum(
                    "hqk,qhd->khd",
                    probs.astype(bf16),
                    context_grad_heads,
                    preferred_element_type=f32,
                )
                key_part = (
                    jnp.einsum("hqk,qhd->khd", score_grad_b, queries, preferred_element_type=f32)
                    * score_scale
                )
                key_grads = add_rows(inner[1], key_part.reshape(count, D), offset)
                value_grads = add_rows(inner[2], value_part.reshape(count, D), offset)
                return (query_grad, key_grads, value_grads)

            return lax.cond(offset <= last_query, backward_visit, lambda inner: inner, carry)

        def backward_piece(carry, piece, start):
            return over_blocks(carry, piece[0], piece[1], tok_rows, backward_block)

        return backward_piece

    query_zero = jnp.zeros((tok_rows, HEADS, HEAD), f32)
    back_fn = make_backward()
    back_init = (query_zero, jnp.zeros((group_rows, D), f32), jnp.zeros((group_rows, D), f32))
    folded = back_fn(
        back_init,
        (
            lax.all_gather(keys_b, "seq", axis=0, tiled=True),
            lax.all_gather(values_b, "seq", axis=0, tiled=True),
        ),
        jnp.int32(0),
    )
    query_grad = folded[0]
    key_grad, value_grad = (
        lax.psum_scatter(
            folded[1].astype(jnp.bfloat16), "seq", scatter_dimension=0, tiled=True
        ).astype(jnp.float32),
        lax.psum_scatter(
            folded[2].astype(jnp.bfloat16), "seq", scatter_dimension=0, tiled=True
        ).astype(jnp.float32),
    )
    query_rot = rotate(query_grad, -positions).reshape(tok_rows, D)
    key_rot = rotate(key_grad.reshape(tok_rows, HEADS, HEAD), -positions).reshape(tok_rows, D)
    proj_grad_b = jnp.concatenate([query_rot, key_rot, value_grad], axis=1).astype(bf16)
    qkv_w_grad = jnp.dot(normed_b.T, proj_grad_b, preferred_element_type=f32)
    normed_grad = jnp.dot(proj_grad_b, weight_qkv.T, preferred_element_type=f32)
    _, first_norm_back = jax.vjp(rms_scale, x_rows, gain_attn)
    x_norm_grad, gain_attn_grad = first_norm_back(normed_grad)
    input_grad = mid_grad + x_norm_grad
    attn_w_grad = jnp.concatenate([qkv_w_grad, out_w_grad], axis=1)
    attn_cols = lax.psum_scatter(
        attn_w_grad.astype(jnp.bfloat16), "seq", scatter_dimension=1, tiled=True
    ).astype(jnp.float32)
    attn_blocks = attn_cols.reshape(D, attn_row, BW).transpose(1, 0, 2)
    expert_grad = jnp.stack([gate_w_grad, up_w_grad, down_w_grad], axis=1)
    nj_count = expert_grad.shape[3] // BW
    expert_blocks = (
        expert_grad.reshape(EXPERTS, 3, D, nj_count, BW).transpose(0, 1, 3, 2, 4).reshape(-1, D, BW)
    )
    row_grads = jnp.concatenate([attn_blocks, expert_blocks], axis=0)
    slotted = jnp.einsum("bi,brc->irc", choose.astype(f32), row_grads, precision=highest)
    owned_grad = lax.psum_scatter(
        slotted.astype(jnp.bfloat16), "dp", scatter_dimension=0, tiled=True
    ).astype(jnp.float32)
    new_masters, new_left, new_right = shampoo_update(
        masters, owned_grad, stat_left, stat_right, root_left, root_right
    )
    small_local = pack_small(
        gain_attn_grad, gain_moe_grad, router_grad, router_prior_grad, mix_grad, value_grad_small
    )
    small_total = lax.psum(small_local, ("seq", "dp"))
    small_now = pack_small(gain_attn, gain_moe, router, router_prior, const_mix, const_value)
    new_small, new_first, new_second = adam_update(small_now, small_total, adam_first, adam_second)
    return (
        block_rows.astype(bf16)[None],
        input_grad[None],
        prior_grad[None],
        owned_grad,
        new_masters,
        new_left,
        new_right,
        small_total,
        new_small,
        new_first,
        new_second,
    )


def solution(mesh):
    in_specs = (
        P("dp", "seq", None),
        P("dp", "seq", None),
        P("dp", "seq", None),
        P("dp", "seq", None),
        P(("seq", "dp"), None, None),
        P("seq", None),
        P(("seq", "dp"), None, None),
        P(("seq", "dp"), None, None),
        P(("seq", "dp"), None, None),
        P(("seq", "dp"), None, None),
        P(),
        P(),
        P(),
        P(),
        P(),
        P(),
        P(),
        P(),
    )
    out_specs = (
        P("dp", "seq", None),
        P("dp", "seq", None),
        P("dp", "seq", None),
        P(("seq", "dp"), None, None),
        P(("seq", "dp"), None, None),
        P(("seq", "dp"), None, None),
        P(("seq", "dp"), None, None),
        P(),
        P(),
        P(),
        P(),
    )
    return jax.shard_map(body, mesh=mesh, in_specs=in_specs, out_specs=out_specs, check_vma=False)
```

profile of v0, /device:TPU:0, one launch (start us, length us, event | category | flops | bytes accessed | tf_op | source)
XLA Modules:
  0.0 1862.3 jit_solution(3686758781759464804)
XLA Ops:
  12.0 77.8 %all_to_all.18 = bf16[13,768,128]{2,0,1:T(8,128)(2,1)S(1)} all-to-all(bf16[13,768,128]{2,0,1:T(8,128)(2,1)S(1)} %copy.225), channel_id=1, replica_groups=mesh['seq'=4,'dp'=8] {'dp'}, dimensions={1} | all-to-all | bytes 5111808 | tf_op jit(solution)/shard_map/all_to_all | solution.py:190
  96.4 60.3 %all-gather.8.cloned.1.call-done = bf16[192,96,128]{2,1,0:T(8,128)(2,1)} async-done(((bf16[6,96,128]{2,1,0:T(8,128)(2,1)}), bf16[192,96,128]{2,1,0:T(8,128)(2,1)}) %all-gather.8.cloned.1.call-update) | async-done | bytes 4718608 | tf_op jit(solution)/shard_map/all_gather | solution.py:196
  156.7 7.1 copy.231
  163.8 10.1 reshape.711
  192.8 23.3 %all-gather.10.cloned.1.call-done = bf16[2048,768]{1,0:T(8,128)(2,1)} async-done(((bf16[512,768]{1,0:T(8,128)(2,1)}), bf16[2048,768]{1,0:T(8,128)(2,1)}) %all-gather.10.cloned.1.call-update) | async-done | bytes 3145744 | tf_op jit(solution)/shard_map/all_gather | solution.py:249
  220.8 26.0 %all-gather.12.cloned.1.call-done = bf16[2048,768]{1,0:T(8,128)(2,1)} async-done(((bf16[512,768]{1,0:T(8,128)(2,1)}), bf16[2048,768]{1,0:T(8,128)(2,1)}) %all-gather.12.cloned.1.call-update) | async-done | bytes 3145744 | tf_op jit(solution)/shard_map/all_gather | solution.py:250
  251.7 16.5 while.32
  252.9 11.4 conditional.6
  278.4 39.7 %all_gather.30 = bf16[2048,2]{1,0:T(8,128)(2,1)S(1)} all-gather(bf16[512,2]{1,0:T(8,128)(2,1)S(1)} %bitcast_convert_fusion), channel_id=1, replica_groups=mesh['seq'=4,'dp'=8] {'seq'}, dimensions={0}, use_global_device_ids=true | all-gather | bytes 10240 | tf_op jit(solution)/shard_map/all_gather | solution.py:271
  327.1 10.9 while.31
  339.7 21.4 %gather_fusion.2 = bf16[4096,768]{1,0:T(8,128)(2,1)} fusion(bf16[2048,768]{1,0:T(8,128)(2,1)} %bitcast.294, s32[4096]{0:T(1024)S(1)} %broadcast_clamp_fusion.1), kind=kCustom, calls=%fused_computation.2 | custom fusion | bytes 12599296 | tf_op jit(solution)/shard_map/gather | solution.py:295
  363.0 8.6 gather_fusion.3
  373.2 7.5 all_gather.33
  381.3 25.6 %gather_fusion.1 = bf16[4096]{0:T(1024)(128)(2,1)S(1)} fusion(bf16[4096]{0:T(1024)(128)(2,1)S(1)} %reshape.719, s32[4096]{0:T(1024)S(1)} %broadcast_clamp_fusion), kind=kCustom, calls=%fused_computation.1 | custom fusion | bytes 32768 | tf_op jit(solution)/shard_map/gather | solution.py:276
  407.1 21.5 %gather_fusion = bf16[4096,768]{1,0:T(8,128)(2,1)} fusion(bf16[2048,768]{1,0:T(8,128)(2,1)} %all-gather.14.cloned.1.call-done, s32[4096]{0:T(1024)S(1)} %broadcast_clamp_fusion.1), kind=kCustom, calls=%fused_computation | custom fusion | bytes 12599296 | tf_op jit(solution)/shard_map/gather | solution.py:277
  428.6 271.9 %all-gather.16.cloned.1.call-done = bf16[96,768,128]{2,0,1:T(8,128)(2,1)} async-done(((bf16[96,96,128]{2,0,1:T(8,128)(2,1)}), bf16[96,768,128]{2,0,1:T(8,128)(2,1)}) %all-gather.16.cloned.1.call-update) | async-done | bytes 18874384 | tf_op jit(solution)/shard_map/all_gather | solution.py:204
  700.5 13.6 copy.337
  714.1 27.8 %reshape.718 = bf16[8,3,768,512]{3,2,0,1:T(8,128)(2,1)} reshape(bf16[8,3,768,4,128]{4,3,2,0,1:T(4,128)(2,1)} %bitcast.299) | data formatting | bytes 37748736 | tf_op jit(solution)/shard_map/reshape | solution.py:89
  741.9 11.9 fusion.35
  753.9 8.4 fusion.33
  762.3 15.5 multiply_convert_fusion
  777.8 11.1 fusion.30
  788.9 30.9 %scatter_custom_fusion = f32[2048,768]{1,0:T(8,128)} fusion(s32[4096]{0:T(1024)} %bitcast.338, f32[4096,768]{1,0:T(8,128)} %bitcast.355, f32[]{:T(128)} %constant.158.clone.1), kind=kCustom, calls=%fused_computation.92 | custom fusion | flops 3145728 | bytes 6291968 | tf_op jit(solution)/shard_map/scatter-add | solution.py:285
  824.7 28.8 %scatter_custom_fusion.1 = f32[4096]{0:T(1024)S(1)} fusion(s32[4096]{0:T(1024)} %bitcast.340, f32[4096]{0:T(1024)S(1)} %bitcast.341, f32[]{:T(128)} %constant.158.clone.1), kind=kCustom, calls=%fused_computation.246 | custom fusion | flops 4096 | bytes 16896 | tf_op jit(solution)/shard_map/scatter-add | solution.py:316
  855.4 12.4 fusion.32
  867.9 16.0 fusion.41
  883.9 30.7 %scatter_custom_fusion.2 = f32[2048,768]{1,0:T(8,128)} fusion(s32[4096]{0:T(1024)} %bitcast.339, f32[4096,768]{1,0:T(8,128)} %bitcast.314, f32[]{:T(128)} %constant.158.clone.1), kind=kCustom, calls=%fused_computation.90 | custom fusion | flops 3145728 | bytes 6291968 | tf_op jit(solution)/shard_map/scatter-add | solution.py:311
  977.4 63.3 %while.33 = (s32[]{:T(128)}, f32[512,12,64]{0,2,1:T(8,128)}, f32[2048,768]{0,1:T(8,128)}, f32[2048,768]{0,1:T(8,128)}, s32[4]{0:T(128)S(1)}, /*index=5*/s32[]{:T...) while((s32[]{:T(128)}, f32[512,12,64]{0,2,1:T(8,128)}, ...), condition=%wide.region_39.40_spmd.clone, body=%wide.region_36.39_spmd.clone.sunk | while | flops 2046952448 | bytes 119624112 | solution.py:106
  978.7 58.3 %conditional.7 = ((f32[512,12,64]{0,2,1:T(8,128)}, f32[2048,768]{0,1:T(8,128)}, f32[2048,768]{0,1:T(8,128)})) conditional(s32[]{:T(128)} %convert_element_type.262, (f32[512,12,64]{0,2,1:T(8,128)}, f32[2048,768]{0,1:T(8,128)}, f32[2048,768]{0,1:T(8,128)}) %tuple.157, (s32[]{:T(128)}, s32[]{:T(128)}, bf16[4,512,768]{1,2,0:T(8,128)(2,1)}, ...), branch_computations={%region_37.37_spmd, %region_38.38_spmd} | conditional | flops 2046952448 | bytes 119621776 | solution.py:382
  979.9 6.6 fusion.149
  988.6 7.1 fusion.15
  1014.4 8.5 dynamic_update_slice.9
  1022.9 8.6 dynamic_update_slice.8
  1053.0 202.8 %reduce-scatter.16.cloned.1.call-done = bf16[512,768]{0,1:T(8,128)(2,1)} async-done(((bf16[2048,768]{0,1:T(8,128)(2,1)}), bf16[512,768]{0,1:T(8,128)(2,1)}) %reduce-scatter.16.cloned.1.call-update) | async-done | bytes 786448 | tf_op jit(solution)/shard_map/reduce_scatter | solution.py:402
  1259.3 37.3 %reduce-scatter.18.cloned.1.call-done = bf16[512,768]{0,1:T(8,128)(2,1)} async-done(((bf16[2048,768]{0,1:T(8,128)(2,1)}), bf16[512,768]{0,1:T(8,128)(2,1)}) %reduce-scatter.18.cloned.1.call-update) | async-done | bytes 786448 | tf_op jit(solution)/shard_map/reduce_scatter | solution.py:405
  1303.1 13.1 fusion.150
  1316.2 9.4 fusion.151
  1325.6 12.3 fusion.38
  1337.9 25.2 %maximum_bitcast_fusion = f32[8,3,4,768,128]{3,4,2,0,1:T(8,128)} fusion(f32[8,1,768,4,128]{2,4,3,0,1:T(8,128)} %bitcast.304, f32[8,1,768,4,128]{2,4,3,0,1:T(8,128)} %bitcast.306, f32[8,1,768,4,128]{2,4,3,0,1:T(8,128)} %bitcast.305), kind=kLoop, calls=%fused_computation.51 | loop fusion | flops 18874368 | bytes 75497472 | tf_op jit(solution)/shard_map/transpose | solution.py:425
  1363.1 43.9 %copy.252 = f32[8,3,4,768,128]{4,2,1,0,3:T(4,128)} copy(f32[8,3,4,768,128]{3,4,2,0,1:T(8,128)} %maximum_bitcast_fusion) | data formatting | bytes 75497472 | tf_op jit(solution)/shard_map/transpose | solution.py:425
  1410.9 32.2 %fusion.27 = bf16[104,768,128]{2,0,1:T(8,128)(2,1)} fusion(f32[96,768,128]{2,0,1:T(8,128)} %bitcast.297, f32[6,768,128]{2,0,1:T(8,128)} %bitcast.313, s32[102]{0:T(128)S(1)} %bitcast.354), kind=kOutput, calls=%fused_computation.56 | convolution fusion | flops 12533966848 | bytes 60555672 | tf_op jit(solution)/shard_map/bi,brc->irc/dot_general | solution.py:428
  1443.2 19.2 %copy.253 = bf16[104,768,128]{2,1,0:T(8,128)(2,1)} copy(bf16[104,768,128]{2,0,1:T(8,128)(2,1)} %fusion.27) | data formatting | bytes 40894464 | tf_op jit(solution)/shard_map/convert_element_type | solution.py:430
  1472.2 6.4 fusion.66
  1478.8 44.3 %psum.7 = f32[15504]{0:T(1024)S(1)} all-reduce(f32[15504]{0:T(1024)S(1)} %concatenate.45), channel_id=1, replica_groups=mesh['seq'=4,'dp'=8] {'seq','dp'}, use_global_device_ids=true, to_apply=%region_49.50 | all-reduce | flops 15504 | bytes 124032 | tf_op jit(solution)/shard_map/psum | solution.py:438
  1527.6 272.2 %reduce-scatter.22.cloned.1.call-done = bf16[13,768,128]{2,1,0:T(8,128)(2,1)} async-done(((bf16[104,768,128]{2,1,0:T(8,128)(2,1)}), bf16[13,768,128]{2,1,0:T(8,128)(2,1)}) %reduce-scatter.22.cloned.1.call-update) | async-done | bytes 2555920
  1799.8 19.6 %fusion.152 = f32[13,128,768]{1,2,0:T(8,128)} fusion(bf16[13,768,128]{2,1,0:T(8,128)(2,1)} %reduce-scatter.22.cloned.1.call-done, f32[13,768,768]{2,1,0:T(8,128)} %param.34), kind=kOutput, calls=%fused_computation.292 | convolution fusion | flops 11777605632 | bytes 38338560 | tf_op jit(solution)/shard_map/sij,sjk->sik/dot_general | solution.py:126
  1819.3 8.9 multiply_subtract_fusion
  1831.1 22.7 %add_multiply_fusion = f32[13,768,768]{2,1,0:T(8,128)} fusion(f32[13,768,768]{2,1,0:T(8,128)} %param.32, bf16[13,768,128]{2,1,0:T(8,128)(2,1)S(1)} %copy-done.5), kind=kOutput, calls=%fused_computation.52 | convolution fusion | flops 1978269696 | bytes 63897600 | tf_op jit(solution)/shard_map/sik,sjk->sij/dot_general | solution.py:120
  (434 shorter events, 230.7 us)
Async XLA Ops:
  7.2 1812.1 %copy-start = (f32[13,128,128]{2,1,0:T(8,128)S(1)}, f32[13,128,128]{2,1,0:T(8,128)}, u32[]{:S(2)}) copy-start(f32[13,128,128]{2,1,0:T(8,128)} %param.35) | copy-start | bytes 2555908
  7.2 149.5 %all-gather.8.cloned.1.call-start = ((), (), s32[]{:S(2)}) async-start(), calls=%async_computation.8 | async-start | bytes 4866048 | tf_op jit(solution)/shard_map/all_gather | solution.py:196
  94.0 122.1 %all-gather.10.cloned.1.call-start = ((), (), s32[]{:S(2)}) async-start(), calls=%async_computation.9 | async-start | bytes 3932160 | tf_op jit(solution)/shard_map/all_gather | solution.py:249
  94.7 79.2 %copy-start.87 = (f32[512]{0:T(512)}, f32[512]{0:T(512)S(1)}, u32[]{:S(2)}) copy-start(f32[512]{0:T(512)S(1)} %fusion.133) | copy-start | bytes 6148
  189.1 57.7 %all-gather.12.cloned.1.call-start = ((), (), s32[]{:S(2)}) async-start(), calls=%async_computation.10 | async-start | bytes 3932160 | tf_op jit(solution)/shard_map/all_gather | solution.py:250
  191.6 148.1 %all-gather.18.cloned.1.call-start = ((), (), s32[]{:S(2)}) async-start(), calls=%async_computation.19 | async-start | bytes 3932160 | tf_op jit(solution)/shard_map/all_gather | solution.py:293
  192.2 214.9 %all-gather.14.cloned.1.call-start = ((), (), s32[]{:S(2)}) async-start(), calls=%async_computation.11 | async-start | bytes 3932160 | tf_op jit(solution)/shard_map/all_gather | solution.py:270
  272.1 89.0 %copy-start.6 = (f32[512,768]{1,0:T(8,128)}, f32[512,768]{1,0:T(8,128)S(1)}, u32[]{:S(2)}) copy-start(f32[512,768]{1,0:T(8,128)S(1)} %get-tuple-element.736) | copy-start | bytes 4718596
  272.7 88.4 %copy-start.45 = (f32[512]{0:T(512)}, f32[512]{0:T(512)S(1)}, u32[]{:S(2)}) copy-start(f32[512]{0:T(512)S(1)} %fusion.134) | copy-start | bytes 6148
  273.8 426.7 %all-gather.16.cloned.1.call-start = ((), (), s32[]{:S(2)}) async-start(), calls=%async_computation.12 | async-start | bytes 21233664 | tf_op jit(solution)/shard_map/all_gather | solution.py:204
  278.1 654.3 %reduce-scatter.10.cloned.1.call-start = ((), (), s32[]{:S(2)}) async-start(), calls=%async_computation.13 | async-start | bytes 3932160 | tf_op jit(solution)/shard_map/reduce_scatter | solution.py:287
  278.3 93.5 %copy-start.21 = (s32[1,512,2]{2,1,0:T(8,128)}, s32[1,512,2]{2,1,0:T(8,128)S(1)}, u32[]{:S(2)}) copy-start(s32[1,512,2]{2,1,0:T(8,128)S(1)} %copy.237) | copy-start | bytes 12292
  339.7 21.5 %copy-start.41 = (f32[768,12]{0,1:T(8,128)S(1)}, f32[768,12]{0,1:T(8,128)}, u32[]{:S(2)}) copy-start(f32[768,12]{0,1:T(8,128)} %param.38) | copy-start | bytes 110596
  339.7 23.1 %copy-start.43 = (f32[1,512,12]{1,0,2:T(1,128)S(1)}, f32[1,512,12]{1,0,2:T(1,128)}, u32[]{:S(2)}) copy-start(f32[1,512,12]{1,0,2:T(1,128)} %param.27) | copy-start | bytes 73732
  339.7 23.1 %copy-start.51 = (f32[12,12]{1,0:T(8,128)S(1)}, f32[12,12]{1,0:T(8,128)}, u32[]{:S(2)}) copy-start(f32[12,12]{1,0:T(8,128)} %param.39) | copy-start | bytes 1732
  372.0 35.0 %copy-start.67 = (f32[512]{0:T(512)}, f32[512]{0:T(512)S(1)}, u32[]{:S(2)}) copy-start(f32[512]{0:T(512)S(1)} %get-tuple-element.687) | copy-start | bytes 6148
  372.3 552.8 %copy-start.72 = (f32[512]{0:T(512)}, f32[512]{0:T(512)S(1)}, u32[]{:S(2)}) copy-start(f32[512]{0:T(512)S(1)} %fusion.108) | copy-start | bytes 6148
  407.1 370.7 %copy-start.56 = (f32[8,512]{1,0:T(8,128)}, f32[8,512]{1,0:T(8,128)S(1)}, u32[]{:S(2)}) copy-start(f32[8,512]{1,0:T(8,128)S(1)} %fusion.123) | copy-start | bytes 49156
  741.9 11.9 copy-start.9
  824.6 113.1 %reduce-scatter.12.cloned.1.call-start = ((), (), s32[]{:S(2)}) async-start(), calls=%async_computation.14 | async-start | bytes 655360 | tf_op jit(solution)/shard_map/reduce_scatter | solution.py:323
  867.8 89.6 %reduce-scatter.14.cloned.1.call-start = ((), (), s32[]{:S(2)}) async-start(), calls=%async_computation.15 | async-start | bytes 3932160 | tf_op jit(solution)/shard_map/reduce_scatter | solution.py:320
  919.4 13.0 copy-start.17
  919.4 336.3 %reduce-scatter.16.cloned.1.call-start = ((), (), s32[]{:S(2)}) async-start(), calls=%async_computation.16 | async-start | bytes 3932160 | tf_op jit(solution)/shard_map/reduce_scatter | solution.py:402
  928.1 23.9 %copy-start.48 = (f32[2,512,2]{1,2,0:T(2,128)}, f32[2,512,2]{1,2,0:T(2,128)S(1)}, u32[]{:S(2)}) copy-start(f32[2,512,2]{1,2,0:T(2,128)S(1)} %get-tuple-element.738) | copy-start | bytes 24580
  930.6 18.0 copy-start.54
  937.5 24.7 %copy-start.58 = (f32[1,512,2]{1,2,0:T(2,128)}, f32[1,512,2]{1,2,0:T(2,128)S(1)}, u32[]{:S(2)}) copy-start(f32[1,512,2]{1,2,0:T(2,128)S(1)} %pad_bitcast_fusion) | copy-start | bytes 12292
  937.5 24.7 %copy-start.60 = (f32[1,512,2]{1,2,0:T(2,128)}, f32[1,512,2]{1,2,0:T(2,128)S(1)}, u32[]{:S(2)}) copy-start(f32[1,512,2]{1,2,0:T(2,128)S(1)} %pad_bitcast_fusion.1) | copy-start | bytes 12292
  937.6 24.6 %copy-start.62 = (f32[1,512,2]{1,2,0:T(2,128)}, f32[1,512,2]{1,2,0:T(2,128)S(1)}, u32[]{:S(2)}) copy-start(f32[1,512,2]{1,2,0:T(2,128)S(1)} %pad_bitcast_fusion.2) | copy-start | bytes 12292
  937.6 24.6 %copy-start.64 = (f32[1,512,2]{1,2,0:T(2,128)}, f32[1,512,2]{1,2,0:T(2,128)S(1)}, u32[]{:S(2)}) copy-start(f32[1,512,2]{1,2,0:T(2,128)S(1)} %pad_bitcast_fusion.3) | copy-start | bytes 12292
  937.7 24.5 %copy-start.68 = (f32[2,512]{1,0:T(2,128)}, f32[2,512]{1,0:T(2,128)S(1)}, u32[]{:S(2)}) copy-start(f32[2,512]{1,0:T(2,128)S(1)} %neg.39) | copy-start | bytes 12292
  948.6 13.7 copy-start.33
  1045.8 250.9 %reduce-scatter.18.cloned.1.call-start = ((), (), s32[]{:S(2)}) async-start(), calls=%async_computation.17 | async-start | bytes 3932160 | tf_op jit(solution)/shard_map/reduce_scatter | solution.py:405
  1050.9 206.2 %copy-start.35 = (f32[512,32]{0,1:T(8,128)S(1)}, f32[512,32]{0,1:T(8,128)}, u32[]{:S(2)}) copy-start(f32[512,32]{0,1:T(8,128)} %get-tuple-element.729) | copy-start | bytes 196612
  1051.0 206.2 %copy-start.36 = (f32[512,32]{0,1:T(8,128)S(1)}, f32[512,32]{0,1:T(8,128)}, u32[]{:S(2)}) copy-start(f32[512,32]{0,1:T(8,128)} %get-tuple-element.730) | copy-start | bytes 196612
  1051.0 356.1 %reduce-scatter.20.cloned.1.call-start = ((), (), s32[]{:S(2)}) async-start(), calls=%async_computation.18 | async-start | bytes 5898240 | tf_op jit(solution)/shard_map/reduce_scatter | solution.py:418
  1257.1 39.5 %copy-start.26 = (bf16[1,512,768]{2,1,0:T(8,128)(2,1)S(1)}, bf16[1,512,768]{2,1,0:T(8,128)(2,1)}, u32[]{:S(2)}) copy-start(bf16[1,512,768]{2,1,0:T(8,128)(2,1)} %param.26) | copy-start | bytes 2359300
  1257.1 39.5 %copy-start.83 = (f32[768]{0:T(1024)S(1)}, f32[768]{0:T(1024)}, u32[]{:S(2)}) copy-start(f32[768]{0:T(1024)} %param.36) | copy-start | bytes 9220
  1257.2 39.5 %copy-start.88 = (f32[512]{0:T(512)S(1)}, f32[512]{0:T(512)}, u32[]{:S(2)}) copy-start(f32[512]{0:T(512)} %copy-done.87) | copy-start | bytes 6148
  1259.2 40.9 %copy-start.31 = (bf16[512,12,64]{0,2,1:T(8,128)(2,1)}, bf16[512,12,64]{0,2,1:T(8,128)(2,1)S(1)}, u32[]{:S(2)}) copy-start(bf16[512,12,64]{0,2,1:T(8,128)(2,1)S(1)} %pad_maximum_fusion.6) | copy-start | bytes 2359300
  1259.3 40.9 %copy-start.32 = (bf16[512,12,64]{0,2,1:T(8,128)(2,1)}, bf16[512,12,64]{0,2,1:T(8,128)(2,1)S(1)}, u32[]{:S(2)}) copy-start(bf16[512,12,64]{0,2,1:T(8,128)(2,1)S(1)} %pad_maximum_fusion.7) | copy-start | bytes 2359300
  1303.0 496.7 %reduce-scatter.22.cloned.1.call-start = ((), (), s32[]{:S(2)}) async-start(), calls=%async_computation.20 | async-start | bytes 23003136
  1303.1 13.1 copy-start.10
  1472.2 50.8 %copy-start.77 = (f32[512]{0:T(512)S(1)}, f32[512]{0:T(512)}, u32[]{:S(2)}) copy-start(f32[512]{0:T(512)} %copy-done.76) | copy-start | bytes 6148
  1472.2 50.8 %copy-start.13 = (f32[512,768]{1,0:T(8,128)S(1)}, f32[512,768]{1,0:T(8,128)}, u32[]{:S(2)}) copy-start(f32[512,768]{1,0:T(8,128)} %copy-done.11) | copy-start | bytes 4718596
  1472.2 50.8 %copy-start.27 = (bf16[1,512,768]{2,1,0:T(8,128)(2,1)S(1)}, bf16[1,512,768]{2,1,0:T(8,128)(2,1)}, u32[]{:S(2)}) copy-start(bf16[1,512,768]{2,1,0:T(8,128)(2,1)} %param.26) | copy-start | bytes 2359300
  1478.7 47.4 %copy-start.66 = (f32[15504]{0:T(1024)S(1)}, f32[15504]{0:T(1024)}, u32[]{:S(2)}) copy-start(f32[15504]{0:T(1024)} %param.42) | copy-start | bytes 186052
  1523.0 296.3 %copy-start.37 = (f32[15504]{0:T(1024)}, f32[15504]{0:T(1024)S(1)}, u32[]{:S(2)}) copy-start(f32[15504]{0:T(1024)S(1)} %psum.7) | copy-start | bytes 186052
  1831.1 22.7 %copy-start.30 = (f32[13,128,128]{2,1,0:T(8,128)S(1)}, f32[13,128,128]{2,1,0:T(8,128)}, u32[]{:S(2)}) copy-start(f32[13,128,128]{2,1,0:T(8,128)} %param.33) | copy-start | bytes 2555908
  (61 other events, 276.9 us)
Sparse Core Ops, SparseCore 0:
  94.2 62.5 all-gather.7
  189.3 26.8 all-gather.9
  218.3 28.4 all-gather.11
  248.2 28.4 all-gather.17
  278.7 57.3 all-gather.13
  338.1 362.3 all-gather.15
  824.7 37.8 reduce-scatter.9
  867.9 21.5 reduce-scatter.11
  919.5 37.7 reduce-scatter.13
  1045.9 209.8 reduce-scatter.15
  1258.9 37.7 reduce-scatter.17
  1303.2 47.8 reduce-scatter.19
  1462.7 337.0 reduce-scatter.21
where the time goes:
time: 1870 us; the launch traced here: 1860 us
  waiting for transfers between devices  900 us (48%)
  local copies, waits for them, and re-layouts  302 us (16%)
  matrix products  269 us (14%)
  other arithmetic  198 us (11%)
  blocking collectives  169 us (9%)
    unnamed x14, waiting for transfers between devices  273 us
    all_gather x1, waiting for transfers between devices, body(): lax.all_gather(own_blocks[attn_row:], 'dp', axis=1, tiled=True)  272 us
    reduce_scatter x1, waiting for transfers between devices, body(): lax.psum_scatter(folded[1].astype(jnp.bfloat16), 'seq', scatter_dimension...  203 us
    all_to_all x1, blocking collectives, body(): lax.all_to_all(masters.astype(bf16), 'dp', split_axis=1, concat_axis=0, t...  77.8 us
    all_gather x1, waiting for transfers between devices, body(): lax.all_gather(own_blocks[:attn_row], ('seq', 'dp'), axis=0, tiled=True)  60.3 us
    psum x1, blocking collectives, body(): small_total = lax.psum(small_local, ('seq', 'dp'))  44.3 us
    transpose x1, local copies, waits for them, and re-layouts, body(): expert_grad.reshape(EXPERTS, 3, D, nj_count, BW).transpose(0, 1, 3, 2, 4)  43.9 us
    all_gather x1, blocking collectives, body(): lax.all_gather(route_rows.astype(bf16), 'seq', axis=0, tiled=True)  39.7 us
  transfers between devices with their start and end apart: 13, of which 8 were waited for; matrix products, arithmetic and copies ran while one was open for 21% of the time, Pallas kernels for 0%

commit v1 on v0

--- a/solution.py
+++ b/solution.py
@@ -1,4 +1,6 @@
 from functools import partial
+
+import numpy as np
 
 import jax
 import jax.numpy as jnp
@@ -153,7 +155,83 @@
     )
 
 
+def snake_ring(mesh, axis):
+    devs = np.asarray(mesh.devices)
+    ax = mesh.axis_names.index(axis)
+    count = devs.shape[ax]
+    line = [devs[(0,) * ax + (i,) + (0,) * (devs.ndim - ax - 1)] for i in range(count)]
+    try:
+        coords = [tuple(int(c) for c in d.coords) + (int(d.core_on_chip),) for d in line]
+    except Exception:
+        return list(range(count))
+    vary = [j for j in range(len(coords[0])) if len({c[j] for c in coords}) > 1]
+    if len(vary) == 1:
+        return sorted(range(count), key=lambda i: coords[i][vary[0]])
+    if len(vary) != 2:
+        return list(range(count))
+    ja, jb = vary
+    vals_a = sorted({c[ja] for c in coords})
+    vals_b = sorted({c[jb] for c in coords})
+    na, nb = len(vals_a), len(vals_b)
+    if na * nb != count:
+        return list(range(count))
+    where = {(vals_a.index(c[ja]), vals_b.index(c[jb])): i for i, c in enumerate(coords)}
+    if nb % 2 == 1 and na % 2 == 0:
+        where = {(b, a): i for (a, b), i in where.items()}
+        na, nb = nb, na
+    if nb % 2 == 1 or na < 2:
+        return list(range(count))
+    cycle = []
+    for b in range(nb):
+        span = range(1, na) if b % 2 == 0 else range(na - 1, 0, -1)
+        cycle += [where[(a, b)] for a in span]
+    cycle += [where[(0, b)] for b in range(nb - 1, -1, -1)]
+    return cycle
+
+
+def ring_position(ring, axis):
+    pos_of = [0] * len(ring)
+    for q, d in enumerate(ring):
+        pos_of[d] = q
+    return jnp.asarray(pos_of, jnp.int32)[lax.axis_index(axis)]
+
+
+def ring_gather(x, ring, axis):
+    count = len(ring)
+    fwd = [(ring[q], ring[(q + 1) % count]) for q in range(count)]
+    bwd = [(ring[(q + 1) % count], ring[q]) for q in range(count)]
+    half = x.shape[1] // 2
+    a, b = x[:, :half], x[:, half:]
+    got_a, got_b = [a], [b]
+    for _ in range(1, count):
+        a = lax.ppermute(a, axis, fwd)
+        b = lax.ppermute(b, axis, bwd)
+        got_a.append(a)
+        got_b.append(b)
+    return jnp.stack(got_a), jnp.stack(got_b)
+
+
+def ring_reduce_scatter(chunks_a, chunks_b, ring, axis):
+    count = len(ring)
+    fwd = [(ring[q], ring[(q + 1) % count]) for q in range(count)]
+    bwd = [(ring[(q + 1) % count], ring[q]) for q in range(count)]
+    me = ring_position(ring, axis)
+    f32 = jnp.float32
+    pick = lambda chunks, q: lax.dynamic_index_in_dim(chunks, q % count, 0, keepdims=False)
+    acc_a = pick(chunks_a, me - 1).astype(f32)
+    acc_b = pick(chunks_b, me + 1).astype(f32)
+    for k in range(1, count):
+        acc_a = lax.ppermute(acc_a.astype(jnp.bfloat16), axis, fwd).astype(f32) + pick(
+            chunks_a, me - 1 - k
+        ).astype(f32)
+        acc_b = lax.ppermute(acc_b.astype(jnp.bfloat16), axis, bwd).astype(f32) + pick(
+            chunks_b, me + 1 + k
+        ).astype(f32)
+    return acc_a, acc_b
+
+
 def body(
+    dp_ring,
     tokens,
     prior_logits,
     routes,
@@ -179,21 +257,55 @@
     seq_count = lax.axis_size("seq")
     dp_count = lax.axis_size("dp")
     seq_rank = lax.axis_index("seq")
+    dp_rank = lax.axis_index("dp")
     tok_rows = tokens.shape[1]
     group_rows = tok_rows * seq_count
     capacity = group_rows // 4
-    row_slots = masters.shape[0] * dp_count
+    n_local = masters.shape[0]
+    row_slots = n_local * dp_count
     attn_row = 4 * D // (BW * seq_count)
+    nj_count = (owner.shape[1] - attn_row) // (3 * EXPERTS)
     score_scale = HEAD ** (-0.5)
     positions = seq_rank * tok_rows + jnp.arange(tok_rows, dtype=jnp.int32)
     last_query = seq_rank * tok_rows + tok_rows - 1
-    row_pieces = lax.all_to_all(masters.astype(bf16), "dp", split_axis=1, concat_axis=0, tiled=True)
-    choose = owner[0][:, None] == jnp.arange(row_slots, dtype=jnp.int32)[None, :]
-    own_blocks = jnp.einsum(
-        "bi,irc->brc", choose.astype(bf16), row_pieces, preferred_element_type=f32
+    me = ring_position(dp_ring, "dp")
+    ring_arr = jnp.asarray(dp_ring, jnp.int32)
+    pos_of = [0] * len(dp_ring)
+    for q, d in enumerate(dp_ring):
+        pos_of[d] = q
+    pos_arr = jnp.asarray(pos_of, jnp.int32)
+
+    slots_local = masters.astype(bf16)
+    got_a, got_b = ring_gather(slots_local, dp_ring, "dp")
+    owner_row = owner[0]
+    slot_dev = owner_row // n_local
+    slot_idx = owner_row % n_local
+    expert_dev = slot_dev[attn_row:]
+    expert_idx = slot_idx[attn_row:]
+    k_a = (me - pos_arr[expert_dev]) % dp_count
+    k_b = (pos_arr[expert_dev] - me) % dp_count
+    span = jnp.arange(row_slots, dtype=jnp.int32)[None, :]
+    pick_a = ((k_a * n_local + expert_idx)[:, None] == span).astype(bf16)
+    pick_b = ((k_b * n_local + expert_idx)[:, None] == span).astype(bf16)
+    half_rows = got_a.shape[2]
+    top = jnp.einsum(
+        "bi,irc->brc", pick_a, got_a.reshape(row_slots, half_rows, BW), preferred_element_type=bf16
+    )
+    bottom = jnp.einsum(
+        "bi,irc->brc", pick_b, got_b.reshape(row_slots, half_rows, BW), preferred_element_type=bf16
+    )
+    expert_blocks = jnp.concatenate([top, bottom], axis=1).reshape(
+        EXPERTS, 3, nj_count, D, BW
+    )
+
+    local_span = jnp.arange(n_local, dtype=jnp.int32)[None, :]
+    attn_sel = (
+        (slot_dev[:attn_row] == dp_rank)[:, None] & (slot_idx[:attn_row][:, None] == local_span)
     ).astype(bf16)
-    shard_rows = own_blocks.shape[1]
-    attn_pieces = lax.all_gather(own_blocks[:attn_row], ("seq", "dp"), axis=0, tiled=True)
+    attn_local = jnp.einsum("bi,irc->brc", attn_sel, slots_local, preferred_element_type=bf16)
+    attn_rows = lax.psum_scatter(attn_local, "dp", scatter_dimension=1, tiled=True)
+    shard_rows = attn_rows.shape[1]
+    attn_pieces = lax.all_gather(attn_rows, ("seq", "dp"), axis=0, tiled=True)
     attn_full = (
         attn_pieces.reshape(seq_count, dp_count, attn_row, shard_rows, BW)
         .transpose(1, 3, 0, 2, 4)
@@ -201,7 +313,6 @@
     )
     weight_qkv = attn_full[:, : 3 * D]
     weight_out = attn_full[:, 3 * D :]
-    expert_w = arrange_experts(lax.all_gather(own_blocks[attn_row:], "dp", axis=1, tiled=True))
     x_rows = tokens[0].astype(f32)
     normed = rms_scale(x_rows, gain_attn)
     normed_b = normed.astype(bf16)
@@ -275,10 +386,13 @@
     token_ids = pair_ids // 2
     slot_gates = jnp.where(valid, group_gates.reshape(-1)[pair_ids].astype(f32), 0.0)
     expert_in = group_in[token_ids]
-    gate_act = jnp.einsum("ecd,edf->ecf", expert_in, expert_w[:, 0], preferred_element_type=f32)
-    up_act = jnp.einsum("ecd,edf->ecf", expert_in, expert_w[:, 1], preferred_element_type=f32)
+    w_gate = expert_blocks[:, 0]
+    w_up = expert_blocks[:, 1]
+    w_down = expert_blocks[:, 2]
+    gate_act = jnp.einsum("ecd,ejdn->ecjn", expert_in, w_gate, preferred_element_type=f32)
+    up_act = jnp.einsum("ecd,ejdn->ecjn", expert_in, w_up, preferred_element_type=f32)
     act_b = (jax.nn.silu(gate_act) * up_act).astype(bf16)
-    expert_out = jnp.einsum("ecf,edf->ecd", act_b, expert_w[:, 2], preferred_element_type=f32)
+    expert_out = jnp.einsum("ecjn,ejdn->ecd", act_b, w_down, preferred_element_type=f32)
     partial_out = (
         jnp.zeros((group_rows, D), f32)
         .at[token_ids.reshape(-1)]
@@ -291,22 +405,37 @@
     grad_b = cotangent[0]
     grad_rows = grad_b.astype(f32)
     group_grad = lax.all_gather(grad_b, "seq", axis=0, tiled=True)
-    back_w = arrange_experts(lax.all_gather(own_blocks[attn_row:], "dp", axis=1, tiled=True))
     slot_grad = group_grad[token_ids].astype(f32)
     out_grad_b = (slot_grad * slot_gates[..., None]).astype(bf16)
     gate_grad_slots = jnp.where(valid, jnp.sum(slot_grad * expert_out, axis=-1), 0.0)
-    act_grad = jnp.einsum("ecd,edf->ecf", out_grad_b, back_w[:, 2], preferred_element_type=f32)
+    act_grad = jnp.einsum("ecd,ejdn->ecjn", out_grad_b, w_down, preferred_element_type=f32)
     sigmoid_gate = jax.nn.sigmoid(gate_act)
     gate_grad_b = (
         act_grad * up_act * sigmoid_gate * (1.0 + gate_act * (1.0 - sigmoid_gate))
     ).astype(bf16)
     up_grad_b = (act_grad * gate_act * sigmoid_gate).astype(bf16)
-    down_w_grad = jnp.einsum("ecf,ecd->edf", act_b, out_grad_b, preferred_element_type=f32)
-    gate_w_grad = jnp.einsum("ecd,ecf->edf", expert_in, gate_grad_b, preferred_element_type=f32)
-    up_w_grad = jnp.einsum("ecd,ecf->edf", expert_in, up_grad_b, preferred_element_type=f32)
+    down_w_grad = jnp.einsum("ecjn,ecd->ejdn", act_b, out_grad_b, preferred_element_type=f32)
+    gate_w_grad = jnp.einsum("ecd,ecjn->ejdn", expert_in, gate_grad_b, preferred_element_type=f32)
+    up_w_grad = jnp.einsum("ecd,ecjn->ejdn", expert_in, up_grad_b, preferred_element_type=f32)
     in_grad = jnp.einsum(
-        "ecf,edf->ecd", gate_grad_b, back_w[:, 0], preferred_element_type=f32
-    ) + jnp.einsum("ecf,edf->ecd", up_grad_b, back_w[:, 1], preferred_element_type=f32)
+        "ecjn,ejdn->ecd", gate_grad_b, w_gate, preferred_element_type=f32
+    ) + jnp.einsum("ecjn,ejdn->ecd", up_grad_b, w_up, preferred_element_type=f32)
+
+    expert_grads = (
+        jnp.stack([gate_w_grad, up_w_grad, down_w_grad], axis=1)
+        .reshape(-1, D, BW)
+        .astype(bf16)
+    )
+    target = ring_arr[:, None] * n_local + jnp.arange(n_local, dtype=jnp.int32)[None, :]
+    place = (owner_row[attn_row:][None, None, :] == target[:, :, None]).astype(bf16)
+    slotted = jnp.einsum(
+        "qib,brc->qirc", place, expert_grads, preferred_element_type=bf16
+    )
+    red_a, red_b = ring_reduce_scatter(
+        slotted[:, :, : D // 2], slotted[:, :, D // 2 :], dp_ring, "dp"
+    )
+    expert_owned = jnp.concatenate([red_a, red_b], axis=1)
+
     token_grad = (
         jnp.zeros((group_rows, D), f32).at[token_ids.reshape(-1)].add(in_grad.reshape(-1, D))
     )
@@ -389,14 +518,7 @@
     query_zero = jnp.zeros((tok_rows, HEADS, HEAD), f32)
     back_fn = make_backward()
     back_init = (query_zero, jnp.zeros((group_rows, D), f32), jnp.zeros((group_rows, D), f32))
-    folded = back_fn(
-        back_init,
-        (
-            lax.all_gather(keys_b, "seq", axis=0, tiled=True),
-            lax.all_gather(values_b, "seq", axis=0, tiled=True),
-        ),
-        jnp.int32(0),
-    )
+    folded = back_fn(back_init, piece, jnp.int32(0))
     query_grad = folded[0]
     key_grad, value_grad = (
         lax.psum_scatter(
@@ -419,23 +541,23 @@
         attn_w_grad.astype(jnp.bfloat16), "seq", scatter_dimension=1, tiled=True
     ).astype(jnp.float32)
     attn_blocks = attn_cols.reshape(D, attn_row, BW).transpose(1, 0, 2)
-    expert_grad = jnp.stack([gate_w_grad, up_w_grad, down_w_grad], axis=1)
-    nj_count = expert_grad.shape[3] // BW
-    expert_blocks = (
-        expert_grad.reshape(EXPERTS, 3, D, nj_count, BW).transpose(0, 1, 3, 2, 4).reshape(-1, D, BW)
-    )
-    row_grads = jnp.concatenate([attn_blocks, expert_blocks], axis=0)
-    slotted = jnp.einsum("bi,brc->irc", choose.astype(f32), row_grads, precision=highest)
-    owned_grad = lax.psum_scatter(
-        slotted.astype(jnp.bfloat16), "dp", scatter_dimension=0, tiled=True
-    ).astype(jnp.float32)
+    attn_sum = lax.psum(attn_blocks.astype(bf16), "dp")
+    owned_grad = expert_owned + jnp.einsum(
+        "bi,brc->irc", attn_sel, attn_sum, preferred_element_type=f32
+    )
     new_masters, new_left, new_right = shampoo_update(
         masters, owned_grad, stat_left, stat_right, root_left, root_right
     )
     small_local = pack_small(
         gain_attn_grad, gain_moe_grad, router_grad, router_prior_grad, mix_grad, value_grad_small
     )
-    small_total = lax.psum(small_local, ("seq", "dp"))
+    small_size = small_local.shape[0]
+    n_dev = seq_count * dp_count
+    small_pad = (-small_size) % n_dev
+    small_part = lax.psum_scatter(
+        jnp.pad(small_local, (0, small_pad)), ("seq", "dp"), scatter_dimension=0, tiled=True
+    )
+    small_total = lax.all_gather(small_part, ("seq", "dp"), axis=0, tiled=True)[:small_size]
     small_now = pack_small(gain_attn, gain_moe, router, router_prior, const_mix, const_value)
     new_small, new_first, new_second = adam_update(small_now, small_total, adam_first, adam_second)
     return (
@@ -487,4 +609,4 @@
         P(),
         P(),
     )
-    return jax.shard_map(body, mesh=mesh, in_specs=in_specs, out_specs=out_specs, check_vma=False)
+    return jax.shard_map(partial(body, snake_ring(mesh, "dp")), mesh=mesh, in_specs=in_specs, out_specs=out_specs, check_vma=False)

time: 1870 us -> 1620 us (0.87)
  waiting for transfers between devices: 900 us -> 529 us
  matrix products: 269 us -> 337 us
  starting transfers between devices: 1.52 us -> 39.8 us
  other arithmetic: 198 us -> 232 us
    all_gather x2 -> x1, waiting for transfers between devices: 332 us -> 58 us  [body(): attn_pieces = lax.all_gather(attn_rows, ('seq', 'dp'), axis=0, tiled=True)]
    unnamed x14 -> x13, waiting for transfers between devices: 273 us -> 0.88 us
    ppermute x0 -> x28, waiting for transfers between devices: none -> 221 us  [the longest x7 122 us: ring_reduce_scatter(): lax.ppermute(acc_b.astype(jnp.bfloat16), axis, bwd).astype(f32)]
    reduce_scatter x1, waiting for transfers between devices: 203 us -> 60 us  [body(): lax.psum_scatter(folded[1].astype(jnp.bfloat16), 'seq', scatter_dimension...]
    unnamed x0 -> x2, blocking collectives: none -> 109 us
    all_to_all x1 -> x0, blocking collectives: 77.8 us -> none  [body(): lax.all_to_all(masters.astype(bf16), 'dp', split_axis=1, concat_axis=0, t...]
    reduce_scatter x0 -> x1, waiting for transfers between devices: none -> 68.5 us  [body(): lax.psum_scatter(attn_local, 'dp', scatter_dimension=1, tiled=True)]
    transpose x3 -> x0, local copies, waits for them, and re-layouts: 47.8 us -> none  [the longest x1 43.9 us: body(): expert_grad.reshape(EXPERTS, 3, D, nj_count, BW).transpose(0, 1, 3, 2, 4)]
  transfers between devices with their start and end apart: 13 -> 41, of which waited for: 8 -> 25; matrix products, arithmetic and copies ran while one was open for 21% -> 32% of each run, Pallas kernels for 0% -> 0%
where the time goes in v1:
time: 1620 us; the launch traced here: 1610 us
  waiting for transfers between devices  529 us (33%)
  matrix products  337 us (21%)
  local copies, waits for them, and re-layouts  284 us (18%)
  other arithmetic  232 us (14%)
  blocking collectives  158 us (10%)
  starting transfers between devices  39.8 us (2%)
  between operations  25.7 us (2%)
    ppermute x7, waiting for transfers between devices, ring_reduce_scatter(): lax.ppermute(acc_b.astype(jnp.bfloat16), axis, bwd).astype(f32)  122 us
    unnamed x2, blocking collectives  109 us
    reduce_scatter x1, waiting for transfers between devices, body(): lax.psum_scatter(folded[2].astype(jnp.bfloat16), 'seq', scatter_dimension...  76 us
    reduce_scatter x1, waiting for transfers between devices, body(): lax.psum_scatter(attn_local, 'dp', scatter_dimension=1, tiled=True)  68.5 us
    ppermute x7, waiting for transfers between devices, ring_gather(): b = lax.ppermute(b, axis, bwd)  68.1 us
    reduce_scatter x1, waiting for transfers between devices, body(): lax.psum_scatter(folded[1].astype(jnp.bfloat16), 'seq', scatter_dimension...  60 us
    all_gather x1, waiting for transfers between devices, body(): attn_pieces = lax.all_gather(attn_rows, ('seq', 'dp'), axis=0, tiled=True)  58 us
    unnamed x262, local copies, waits for them, and re-layouts  56 us
  transfers between devices with their start and end apart: 41, of which 25 were waited for; matrix products, arithmetic and copies ran while one was open for 32% of the time, Pallas kernels for 0%

profile of v1, /device:TPU:0, one launch (start us, length us, event | category | flops | bytes accessed | tf_op | source)
XLA Modules:
  0.0 1613.2 jit_solution(13372736034908506206)
XLA Ops:
  13.6 68.5 %reduce-scatter.8.cloned.1.call-done = bf16[6,96,128]{2,0,1:T(8,128)(2,1)} async-done(((bf16[6,768,128]{2,0,1:T(8,128)(2,1)}), bf16[6,96,128]{2,0,1:T(8,128)(2,1)}) %reduce-scatter.8.cloned.1.call-update) | async-done | bytes 147472 | tf_op jit(solution)/shard_map/reduce_scatter | solution.py:306
  91.3 58.0 %all-gather.7.cloned.1.call-done = bf16[192,96,128]{2,1,0:T(8,128)(2,1)} async-done(((bf16[6,96,128]{2,1,0:T(8,128)(2,1)}), bf16[192,96,128]{2,1,0:T(8,128)(2,1)}) %all-gather.7.cloned.1.call-update) | async-done | bytes 4718608 | tf_op jit(solution)/shard_map/all_gather | solution.py:308
  156.4 10.3 reshape.797
  184.1 28.6 %collective-permute-done.8 = bf16[13,384,128]{2,1,0:T(8,128)(2,1)} collective-permute-done((bf16[13,384,128]{2,1,0:T(8,128)(2,1)}, bf16[13,384,128]{2,1,0:T(8,128)(2,1)}, u32[]{:S(2)}, u32[]{:S(2)}) %collective-permute-start.8) | collective-permute-done | bytes 1277984 | tf_op jit(solution)/shard_map/ppermute | solution.py:208
  229.6 10.9 while.31
  254.7 16.9 %collective-permute-done.10 = bf16[13,384,128]{2,1,0:T(8,128)(2,1)} collective-permute-done((bf16[13,384,128]{2,1,0:T(8,128)(2,1)}, bf16[13,384,128]{2,1,0:T(8,128)(2,1)}, u32[]{:S(2)}, u32[]{:S(2)}) %collective-permute-start.10) | collective-permute-done | bytes 1277984 | tf_op jit(solution)/shard_map/ppermute | solution.py:208
  318.8 21.5 %gather_fusion.2 = bf16[4096,768]{1,0:T(8,128)(2,1)} fusion(bf16[2048,768]{1,0:T(8,128)(2,1)} %bitcast.470, s32[4096]{0:T(1024)S(1)} %broadcast_clamp_fusion.1), kind=kCustom, calls=%fused_computation.2 | custom fusion | bytes 12599296 | tf_op jit(solution)/shard_map/gather | solution.py:408
  357.1 13.4 collective-permute-done.13
  386.0 18.4 %while.32 = (s32[]{:T(128)}, f32[12,512]{1,0:T(8,128)S(1)}, f32[12,512]{1,0:T(8,128)S(1)}, f32[12,512,64]{1,2,0:T(8,128)}, s32[4]{0:T(128)S(1)}, /*index=5*/s32[...) while((s32[]{:T(128)}, f32[12,512]{1,0:T(8,128)S(1)}, ...), condition=%wide.region_7.8_spmd.clone, body=%wide.region_2.7_spmd.clone.sunk | while | flops 847262720 | bytes 47853856 | solution.py:108
  387.2 13.2 conditional.6
  410.8 8.8 reduce-scatter.10.cloned.1.call-start
  419.6 15.5 fusion.28
  435.0 15.8 fusion.30
  450.8 12.9 pad_maximum_fusion
  484.2 41.9 %all_gather.29 = bf16[2048,2]{1,0:T(8,128)(2,1)S(1)} all-gather(bf16[512,2]{1,0:T(8,128)(2,1)S(1)} %get-tuple-element.683), channel_id=1, replica_groups=mesh['seq'=4,'dp'=8] {'seq'}, dimensions={0}, use_global_device_ids=true | all-gather | bytes 10240 | tf_op jit(solution)/shard_map/all_gather | solution.py:383
  526.7 26.0 %gather_fusion.1 = bf16[4096]{0:T(1024)(128)(2,1)S(1)} fusion(bf16[4096]{0:T(1024)(128)(2,1)S(1)} %reshape.806, s32[4096]{0:T(1024)S(1)} %copy-done.69), kind=kCustom, calls=%fused_computation.1 | custom fusion | bytes 32768 | tf_op jit(solution)/shard_map/gather | solution.py:387
  552.9 21.4 %gather_fusion = bf16[4096,768]{1,0:T(8,128)(2,1)} fusion(bf16[2048,768]{1,0:T(8,128)(2,1)} %all-gather.13.cloned.1.call-done, s32[4096]{0:T(1024)S(1)} %copy-done.56), kind=kCustom, calls=%fused_computation | custom fusion | bytes 12599296 | tf_op jit(solution)/shard_map/gather | solution.py:388
  574.3 11.7 fusion.34
  586.0 9.4 fusion.36
  595.4 18.0 %multiply_convert_fusion = (bf16[8,512,4,128]{3,1,2,0:T(8,128)(2,1)}, bf16[8,512,4,128]{3,1,2,0:T(8,128)(2,1)}, bf16[8,512,4,128]{3,1,2,0:T(8,128)(2,1)}) fusion(f32[8,512,4,128]{3,1,2,0:T(8,128)} %fusion.34, f32[8,512,4,128]{3,1,2,0:T(8,128)} %fusion.36, bf16[8,1,4,768,128]{4,2,1,0,3:T(4,128)(2,1)} %get-tuple-element.702, ...), kind=kOutput, calls=%fused_computation.63 | convolution fusion | flops 3264217088 | bytes 41959424 | tf_op jit(solution)/shard_map/ecd,ejdn->ecjn/dot_general | solution.py:411
  613.4 14.7 fusion.26
  628.2 30.5 %scatter_custom_fusion = f32[2048,768]{1,0:T(8,128)} fusion(s32[4096]{0:T(1024)} %bitcast.510, f32[4096,768]{1,0:T(8,128)} %bitcast.527, f32[]{:T(128)} %constant.345.clone.1), kind=kCustom, calls=%fused_computation.101 | custom fusion | flops 3145728 | bytes 6291968 | tf_op jit(solution)/shard_map/scatter-add | solution.py:399
  663.6 29.0 %scatter_custom_fusion.1 = f32[4096]{0:T(1024)S(1)} fusion(s32[4096]{0:T(1024)} %bitcast.512, f32[4096]{0:T(1024)S(1)} %bitcast.513, f32[]{:T(128)} %constant.345.clone.1), kind=kCustom, calls=%fused_computation.316 | custom fusion | flops 4096 | bytes 16896 | tf_op jit(solution)/shard_map/scatter-add | solution.py:445
  694.5 12.9 fusion.33
  707.5 17.0 %bitcast_add_fusion.3 = f32[8,512,768]{2,1,0:T(8,128)} fusion(f32[8,512,768,1]{2,1,3,0:T(8,128)} %fusion.33, bf16[8,512,4,128]{3,1,2,0:T(8,128)(2,1)} %get-tuple-element.705, bf16[8,1,4,768,128]{4,2,1,0,3:T(4,128)(2,1)} %get-tuple-element.703), kind=kOutput, calls=%fused_computation.57 | convolution fusion | flops 3224371200 | bytes 35651584 | tf_op jit(solution)/shard_map/ecjn,ejdn->ecd/dot_general | solution.py:422
  724.5 30.9 %scatter_custom_fusion.2 = f32[2048,768]{1,0:T(8,128)} fusion(s32[4096]{0:T(1024)} %bitcast.511, f32[4096,768]{1,0:T(8,128)} %bitcast.475, f32[]{:T(128)} %constant.345.clone.1), kind=kCustom, calls=%fused_computation.99 | custom fusion | flops 3145728 | bytes 6291968 | tf_op jit(solution)/shard_map/scatter-add | solution.py:440
  816.3 63.8 %while.33 = (s32[]{:T(128)}, f32[512,12,64]{0,2,1:T(8,128)}, f32[2048,768]{0,1:T(8,128)}, f32[2048,768]{0,1:T(8,128)}, s32[4]{0:T(128)S(1)}, /*index=5*/s32[]{:T...) while((s32[]{:T(128)}, f32[512,12,64]{0,2,1:T(8,128)}, ...), condition=%wide.region_40.41_spmd.clone, body=%wide.region_37.40_spmd.clone.sunk | while | flops 2046952448 | bytes 119624120 | solution.py:108
  817.7 58.5 %conditional.7 = ((f32[512,12,64]{0,2,1:T(8,128)}, f32[2048,768]{0,1:T(8,128)}, f32[2048,768]{0,1:T(8,128)})) conditional(s32[]{:T(128)} %convert_element_type.530, (f32[512,12,64]{0,2,1:T(8,128)}, f32[2048,768]{0,1:T(8,128)}, f32[2048,768]{0,1:T(8,128)}) %tuple.179, (s32[]{:T(128)}, s32[]{:T(128)}, bf16[4,512,768]{1,2,0:T(8,128)(2,1)}, ...), branch_computations={%region_38.38_spmd, %region_39.39_spmd} | conditional | flops 2046952448 | bytes 119621776 | solution.py:511
  895.5 10.3 convert_bitcast_fusion.1
  911.4 10.2 convert_bitcast_fusion
  921.5 15.1 pad_maximum_fusion.1
  936.6 24.6 %copy.359 = bf16[8,3,4,768,128]{4,3,2,1,0:T(8,128)(2,1)} copy(bf16[8,3,4,768,128]{3,4,2,0,1:T(8,128)(2,1)} %pad_maximum_fusion.1) | data formatting | bytes 37748736 | tf_op jit(solution)/shard_map/stack | solution.py:425
  966.6 25.1 %fusion.23 = bf16[8,13,768,128]{3,1,2,0:T(8,128)(2,1)} fusion(bf16[96,768,128]{2,1,0:T(8,128)(2,1)} %bitcast.478, s32[8,13]{1,0:T(8,128)S(1)} %iota_add_fusion.3, s32[96]{0:T(128)S(1)} %slice_bitcast_fusion.2), kind=kOutput, calls=%fused_computation.50 | convolution fusion | flops 1962944256 | bytes 39322400 | tf_op jit(solution)/shard_map/qib,brc->qirc/dot_general | solution.py:431
  991.6 10.6 fusion.176
  1014.9 10.6 collective-permute-done.21
  1035.7 60.0 %reduce-scatter.16.cloned.1.call-done = bf16[512,768]{0,1:T(8,128)(2,1)} async-done(((bf16[2048,768]{0,1:T(8,128)(2,1)}), bf16[512,768]{0,1:T(8,128)(2,1)}) %reduce-scatter.16.cloned.1.call-update) | async-done | bytes 786448 | tf_op jit(solution)/shard_map/reduce_scatter | solution.py:524
  1100.8 76.0 %reduce-scatter.18.cloned.1.call-done = bf16[512,768]{0,1:T(8,128)(2,1)} async-done(((bf16[2048,768]{0,1:T(8,128)(2,1)}), bf16[512,768]{0,1:T(8,128)(2,1)}) %reduce-scatter.18.cloned.1.call-update) | async-done | bytes 786448 | tf_op jit(solution)/shard_map/reduce_scatter | solution.py:527
  1190.0 25.8 %collective-permute-done.23 = bf16[13,384,128]{2,1,0:T(8,128)(2,1)S(1)} collective-permute-done((bf16[13,384,128]{2,1,0:T(8,128)(2,1)S(1)}, bf16[13,384,128]{2,1,0:T(8,128)(2,1)S(1)}, u32[]{:S(2)}, u32[]{:S(2)}) %collective-permute-start.23) | collective-permute-done | bytes 1277984 | tf_op jit(solution)/shard_map/ppermute | solution.py:227
  1220.0 25.1 %collective-permute-done.24 = bf16[13,384,128]{2,1,0:T(8,128)(2,1)S(1)} collective-permute-done((bf16[13,384,128]{2,1,0:T(8,128)(2,1)S(1)}, bf16[13,384,128]{2,1,0:T(8,128)(2,1)S(1)}, u32[]{:S(2)}, u32[]{:S(2)}) %collective-permute-start.24) | collective-permute-done | bytes 1277984 | tf_op jit(solution)/shard_map/ppermute | solution.py:227
  1249.1 24.4 %collective-permute-done.25 = bf16[13,384,128]{2,1,0:T(8,128)(2,1)S(1)} collective-permute-done((bf16[13,384,128]{2,1,0:T(8,128)(2,1)S(1)}, bf16[13,384,128]{2,1,0:T(8,128)(2,1)S(1)}, u32[]{:S(2)}, u32[]{:S(2)}) %collective-permute-start.25) | collective-permute-done | bytes 1277984 | tf_op jit(solution)/shard_map/ppermute | solution.py:227
  1281.7 20.8 %collective-permute-done.26 = bf16[13,384,128]{2,1,0:T(8,128)(2,1)} collective-permute-done((bf16[13,384,128]{2,1,0:T(8,128)(2,1)}, bf16[13,384,128]{2,1,0:T(8,128)(2,1)}, u32[]{:S(2)}, u32[]{:S(2)}) %collective-permute-start.26) | collective-permute-done | bytes 1277984 | tf_op jit(solution)/shard_map/ppermute | solution.py:227
  1316.4 15.5 collective-permute-done.27
  1345.0 66.5 %all-reduce.13 = f32[15520]{0:T(1024)S(1)} all-reduce(f32[15520]{0:T(1024)S(1)} %pad.45), channel_id=10, replica_groups=mesh['seq'=4,'dp'=8] {'seq','dp'}, use_global_device_ids=true, to_apply=%region_50.51.clone | all-reduce | flops 15520 | bytes 124160
  1417.1 42.1 %all-reduce.12 = f32[15520]{0:T(1024)S(1)} all-reduce(f32[15520]{0:T(1024)S(1)} %dynamic-slice_dynamic-update-slice_fusion), channel_id=1, replica_groups=mesh['seq'=4,'dp'=8] {'seq','dp'}, use_global_device_ids=true, to_apply=%add.12 | all-reduce | flops 15520 | bytes 124160
  1463.0 44.1 %all-reduce.16.cloned.1.call-done = bf16[6,768,128]{2,0,1:T(8,128)(2,1)} async-done(((bf16[6,768,128]{2,0,1:T(8,128)(2,1)}), bf16[6,768,128]{2,0,1:T(8,128)(2,1)}) %all-reduce.16.cloned.1.call-update) | async-done | bytes 1179664 | tf_op jit(solution)/shard_map/psum | solution.py:544
  1516.0 31.9 %fusion.184 = f32[13,128,768]{1,2,0:T(8,128)} fusion(f32[13,768,128]{2,1,0:T(8,128)S(1)} %maximum_add_fusion, f32[13,768,768]{2,1,0:T(8,128)} %param.38), kind=kOutput, calls=%fused_computation.413 | convolution fusion | flops 11777605632 | bytes 40894464 | tf_op jit(solution)/shard_map/sij,sjk->sik/dot_general | solution.py:128
  1547.9 37.3 %add_multiply_fusion = f32[13,768,768]{2,1,0:T(8,128)} fusion(f32[13,768,768]{2,1,0:T(8,128)} %param.36, f32[13,768,128]{2,1,0:T(8,128)} %copy-done.2), kind=kOutput, calls=%fused_computation.47 | convolution fusion | flops 11792941056 | bytes 66453504 | tf_op jit(solution)/shard_map/sik,sjk->sij/dot_general | solution.py:122
  1585.2 13.2 fusion.101
  (578 shorter events, 457.1 us)
Async XLA Ops:
  7.2 1591.2 %copy-start = (f32[13,128,128]{2,1,0:T(8,128)S(1)}, f32[13,128,128]{2,1,0:T(8,128)}, u32[]{:S(2)}) copy-start(f32[13,128,128]{2,1,0:T(8,128)} %param.39) | copy-start | bytes 2555908
  7.2 74.9 %reduce-scatter.8.cloned.1.call-start = ((), (), s32[]{:S(2)}) async-start(), calls=%async_computation.7 | async-start | bytes 1769472 | tf_op jit(solution)/shard_map/reduce_scatter | solution.py:306
  10.3 265.9 %copy-start.100 = (s32[102]{0:T(128)}, s32[102]{0:T(128)S(1)}, u32[]{:S(2)}) copy-start(s32[102]{0:T(128)S(1)} %get-tuple-element.764) | copy-start | bytes 1228
  13.6 135.7 %all-gather.7.cloned.1.call-start = ((), (), s32[]{:S(2)}) async-start(), calls=%async_computation.8 | async-start | bytes 4866048 | tf_op jit(solution)/shard_map/all_gather | solution.py:308
  83.7 235.1 %all-gather.15.cloned.1.call-start = ((), (), s32[]{:S(2)}) async-start(), calls=%async_computation.19 | async-start | bytes 3932160 | tf_op jit(solution)/shard_map/all_gather | solution.py:407
  84.5 290.8 %all-gather.9.cloned.1.call-start = ((), (), s32[]{:S(2)}) async-start(), calls=%async_computation.9 | async-start | bytes 3932160 | tf_op jit(solution)/shard_map/all_gather | solution.py:360
  86.2 95.8 %collective-permute-start.7 = (bf16[13,384,128]{2,1,0:T(8,128)(2,1)}, bf16[13,384,128]{2,1,0:T(8,128)(2,1)}, u32[]{:S(2)}, u32[]{:S(2)}) collective-permute-start(bf16[13,384,128]{2,1,0:T(8,128)(2,1)} %get-tuple-element.729), channel_id=1, source_target_pairs={{3,1},{5,3},{7,5},{6,7},{4,6},{2,4},{0,2},{1,0},{11,9},{13,11},{15... | collective-permute-start | bytes 3833864 | tf_op jit(solution)/shard_map/ppermute | solution.py:208
  87.2 96.3 %collective-permute-start = (bf16[13,384,128]{2,1,0:T(8,128)(2,1)}, bf16[13,384,128]{2,1,0:T(8,128)(2,1)}, u32[]{:S(2)}, u32[]{:S(2)}) collective-permute-start(bf16[13,384,128]{2,1,0:T(8,128)(2,1)} %get-tuple-element.728), channel_id=1, source_target_pairs={{1,3},{3,5},{5,7},{7,6},{6,4},{4,2},{2,0},{0,1},{9,11},{11,13},{13... | collective-permute-start | bytes 3833864 | tf_op jit(solution)/shard_map/ppermute | solution.py:207
  181.9 198.1 %all-gather.11.cloned.1.call-start = ((), (), s32[]{:S(2)}) async-start(), calls=%async_computation.10 | async-start | bytes 3932160 | tf_op jit(solution)/shard_map/all_gather | solution.py:361
  182.0 30.7 %collective-permute-start.8 = (bf16[13,384,128]{2,1,0:T(8,128)(2,1)}, bf16[13,384,128]{2,1,0:T(8,128)(2,1)}, u32[]{:S(2)}, u32[]{:S(2)}) collective-permute-start(bf16[13,384,128]{2,1,0:T(8,128)(2,1)} %collective-permute-done.7), channel_id=1, source_target_pairs={{3,1},{5,3},{7,5},{6,7},{4,6},{2,4},{0,2},{1,0},{11,9},{13,11},{15... | collective-permute-start | bytes 3833864 | tf_op jit(solution)/shard_map/ppermute | solution.py:208
  183.4 39.1 %collective-permute-start.1 = (bf16[13,384,128]{2,1,0:T(8,128)(2,1)}, bf16[13,384,128]{2,1,0:T(8,128)(2,1)}, u32[]{:S(2)}, u32[]{:S(2)}) collective-permute-start(bf16[13,384,128]{2,1,0:T(8,128)(2,1)} %collective-permute-done), channel_id=1, source_target_pairs={{1,3},{3,5},{5,7},{7,6},{6,4},{4,2},{2,0},{0,1},{9,11},{11,13},{13... | collective-permute-start | bytes 3833864 | tf_op jit(solution)/shard_map/ppermute | solution.py:207
  212.7 29.8 %collective-permute-start.9 = (bf16[13,384,128]{2,1,0:T(8,128)(2,1)}, bf16[13,384,128]{2,1,0:T(8,128)(2,1)}, u32[]{:S(2)}, u32[]{:S(2)}) collective-permute-start(bf16[13,384,128]{2,1,0:T(8,128)(2,1)} %collective-permute-done.8), channel_id=1, source_target_pairs={{3,1},{5,3},{7,5},{6,7},{4,6},{2,4},{0,2},{1,0},{11,9},{13,11},{15... | collective-permute-start | bytes 3833864 | tf_op jit(solution)/shard_map/ppermute | solution.py:208
  222.5 30.8 %collective-permute-start.2 = (bf16[13,384,128]{2,1,0:T(8,128)(2,1)}, bf16[13,384,128]{2,1,0:T(8,128)(2,1)S(1)}, u32[]{:S(2)}, u32[]{:S(2)}) collective-permute-start(bf16[13,384,128]{2,1,0:T(8,128)(2,1)} %collective-permute-done.1), channel_id=1, source_target_pairs={{1,3},{3,5},{5,7},{7,6},{6,4},{4,2},{2,0},{0,1},{9,11},{11,13},{13... | collective-permute-start | bytes 3833864 | tf_op jit(solution)/shard_map/ppermute | solution.py:207
  241.2 77.6 %copy-start.55 = (s32[4096]{0:T(1024)}, s32[4096]{0:T(1024)S(1)}, u32[]{:S(2)}) copy-start(s32[4096]{0:T(1024)S(1)} %broadcast_clamp_fusion.1) | copy-start | bytes 49156
  242.4 29.2 %collective-permute-start.10 = (bf16[13,384,128]{2,1,0:T(8,128)(2,1)}, bf16[13,384,128]{2,1,0:T(8,128)(2,1)}, u32[]{:S(2)}, u32[]{:S(2)}) collective-permute-start(bf16[13,384,128]{2,1,0:T(8,128)(2,1)} %collective-permute-done.9), channel_id=1, source_target_pairs={{3,1},{5,3},{7,5},{6,7},{4,6},{2,4},{0,2},{1,0},{11,9},{13,11},{15... | collective-permute-start | bytes 3833864 | tf_op jit(solution)/shard_map/ppermute | solution.py:208
  253.4 29.7 %collective-permute-start.3 = (bf16[13,384,128]{2,1,0:T(8,128)(2,1)S(1)}, bf16[13,384,128]{2,1,0:T(8,128)(2,1)}, u32[]{:S(2)}, u32[]{:S(2)}) collective-permute-start(bf16[13,384,128]{2,1,0:T(8,128)(2,1)S(1)} %collective-permute-done.2), channel_id=1, source_target_pairs={{1,3},{3,5},{5,7},{7,6},{6,4},{4,2},{2,0},{0,1},{9,11},{11,13},{13... | collective-permute-start | bytes 3833864 | tf_op jit(solution)/shard_map/ppermute | solution.py:207
  271.7 28.4 %collective-permute-start.11 = (bf16[13,384,128]{2,1,0:T(8,128)(2,1)}, bf16[13,384,128]{2,1,0:T(8,128)(2,1)}, u32[]{:S(2)}, u32[]{:S(2)}) collective-permute-start(bf16[13,384,128]{2,1,0:T(8,128)(2,1)} %collective-permute-done.10), channel_id=1, source_target_pairs={{3,1},{5,3},{7,5},{6,7},{4,6},{2,4},{0,2},{1,0},{11,9},{13,11},{15... | collective-permute-start | bytes 3833864 | tf_op jit(solution)/shard_map/ppermute | solution.py:208
  276.1 276.8 %all-gather.13.cloned.1.call-start = ((), (), s32[]{:S(2)}) async-start(), calls=%async_computation.11 | async-start | bytes 3932160 | tf_op jit(solution)/shard_map/all_gather | solution.py:381
  283.1 29.0 %collective-permute-start.4 = (bf16[13,384,128]{2,1,0:T(8,128)(2,1)}, bf16[13,384,128]{2,1,0:T(8,128)(2,1)}, u32[]{:S(2)}, u32[]{:S(2)}) collective-permute-start(bf16[13,384,128]{2,1,0:T(8,128)(2,1)} %collective-permute-done.3), channel_id=1, source_target_pairs={{1,3},{3,5},{5,7},{7,6},{6,4},{4,2},{2,0},{0,1},{9,11},{11,13},{13... | collective-permute-start | bytes 3833864 | tf_op jit(solution)/shard_map/ppermute | solution.py:207
  300.0 42.7 %collective-permute-start.12 = (bf16[13,384,128]{2,1,0:T(8,128)(2,1)}, bf16[13,384,128]{2,1,0:T(8,128)(2,1)}, u32[]{:S(2)}, u32[]{:S(2)}) collective-permute-start(bf16[13,384,128]{2,1,0:T(8,128)(2,1)} %collective-permute-done.11), channel_id=1, source_target_pairs={{3,1},{5,3},{7,5},{6,7},{4,6},{2,4},{0,2},{1,0},{11,9},{13,11},{15... | collective-permute-start | bytes 3833864 | tf_op jit(solution)/shard_map/ppermute | solution.py:208
  312.1 34.5 %collective-permute-start.5 = (bf16[13,384,128]{2,1,0:T(8,128)(2,1)}, bf16[13,384,128]{2,1,0:T(8,128)(2,1)}, u32[]{:S(2)}, u32[]{:S(2)}) collective-permute-start(bf16[13,384,128]{2,1,0:T(8,128)(2,1)} %collective-permute-done.4), channel_id=1, source_target_pairs={{1,3},{3,5},{5,7},{7,6},{6,4},{4,2},{2,0},{0,1},{9,11},{11,13},{13... | collective-permute-start | bytes 3833864 | tf_op jit(solution)/shard_map/ppermute | solution.py:207
  342.7 27.8 %collective-permute-start.13 = (bf16[13,384,128]{2,1,0:T(8,128)(2,1)}, bf16[13,384,128]{2,1,0:T(8,128)(2,1)S(1)}, u32[]{:S(2)}, u32[]{:S(2)}) collective-permute-start(bf16[13,384,128]{2,1,0:T(8,128)(2,1)} %collective-permute-done.12), channel_id=1, source_target_pairs={{3,1},{5,3},{7,5},{6,7},{4,6},{2,4},{0,2},{1,0},{11,9},{13,11},{15... | collective-permute-start | bytes 3833864 | tf_op jit(solution)/shard_map/ppermute | solution.py:208
  346.6 27.5 %collective-permute-start.6 = (bf16[13,384,128]{2,1,0:T(8,128)(2,1)}, bf16[13,384,128]{2,1,0:T(8,128)(2,1)S(1)}, u32[]{:S(2)}, u32[]{:S(2)}) collective-permute-start(bf16[13,384,128]{2,1,0:T(8,128)(2,1)} %collective-permute-done.5), channel_id=1, source_target_pairs={{1,3},{3,5},{5,7},{7,6},{6,4},{4,2},{2,0},{0,1},{9,11},{11,13},{13... | collective-permute-start | bytes 3833864 | tf_op jit(solution)/shard_map/ppermute | solution.py:207
  410.8 363.5 %reduce-scatter.10.cloned.1.call-start = ((), (), s32[]{:S(2)}) async-start(), calls=%async_computation.12 | async-start | bytes 3932160 | tf_op jit(solution)/shard_map/reduce_scatter | solution.py:401
  483.3 283.1 %copy-start.85 = (f32[512]{0:T(512)}, f32[512]{0:T(512)S(1)}, u32[]{:S(2)}) copy-start(f32[512]{0:T(512)S(1)} %fusion.119) | copy-start | bytes 6148
  663.4 115.9 %reduce-scatter.12.cloned.1.call-start = ((), (), s32[]{:S(2)}) async-start(), calls=%async_computation.13 | async-start | bytes 655360 | tf_op jit(solution)/shard_map/reduce_scatter | solution.py:452
  707.4 89.4 %reduce-scatter.14.cloned.1.call-start = ((), (), s32[]{:S(2)}) async-start(), calls=%async_computation.14 | async-start | bytes 3932160 | tf_op jit(solution)/shard_map/reduce_scatter | solution.py:449
  760.2 335.4 %reduce-scatter.16.cloned.1.call-start = ((), (), s32[]{:S(2)}) async-start(), calls=%async_computation.15 | async-start | bytes 3932160 | tf_op jit(solution)/shard_map/reduce_scatter | solution.py:524
  885.1 291.7 %reduce-scatter.18.cloned.1.call-start = ((), (), s32[]{:S(2)}) async-start(), calls=%async_computation.16 | async-start | bytes 3932160 | tf_op jit(solution)/shard_map/reduce_scatter | solution.py:527
  966.1 445.4 %reduce-scatter.20.cloned.1.call-start = ((), (), s32[]{:S(2)}) async-start(), calls=%async_computation.17 | async-start | bytes 5898240 | tf_op jit(solution)/shard_map/reduce_scatter | solution.py:540
  1008.2 17.3 %collective-permute-start.21 = (bf16[13,384,128]{2,1,0:T(8,128)(2,1)S(1)}, bf16[13,384,128]{2,1,0:T(8,128)(2,1)S(1)}, u32[]{:S(2)}, u32[]{:S(2)}) collective-permute-start(bf16[13,384,128]{2,1,0:T(8,128)(2,1)S(1)} %bitcast.498), channel_id=1, source_target_pairs={{3,1},{5,3},{7,5},{6,7},{4,6},{2,4},{0,2},{1,0},{11,9},{13,11},{15... | collective-permute-start | bytes 3833864 | tf_op jit(solution)/shard_map/ppermute | solution.py:227
  1014.3 17.3 %collective-permute-start.14 = (bf16[13,384,128]{2,1,0:T(8,128)(2,1)S(1)}, bf16[13,384,128]{2,1,0:T(8,128)(2,1)S(1)}, u32[]{:S(2)}, u32[]{:S(2)}) collective-permute-start(bf16[13,384,128]{2,1,0:T(8,128)(2,1)S(1)} %bitcast.499), channel_id=1, source_target_pairs={{1,3},{3,5},{5,7},{7,6},{6,4},{4,2},{2,0},{0,1},{9,11},{11,13},{13... | collective-permute-start | bytes 3833864 | tf_op jit(solution)/shard_map/ppermute | solution.py:224
  1027.0 156.7 %collective-permute-start.22 = (bf16[13,384,128]{2,1,0:T(8,128)(2,1)}, bf16[13,384,128]{2,1,0:T(8,128)(2,1)}, u32[]{:S(2)}, u32[]{:S(2)}) collective-permute-start(bf16[13,384,128]{2,1,0:T(8,128)(2,1)} %fusion.59), channel_id=1, source_target_pairs={{3,1},{5,3},{7,5},{6,7},{4,6},{2,4},{0,2},{1,0},{11,9},{13,11},{15... | collective-permute-start | bytes 3833864 | tf_op jit(solution)/shard_map/ppermute | solution.py:227
  1033.2 154.5 %collective-permute-start.15 = (bf16[13,384,128]{2,1,0:T(8,128)(2,1)}, bf16[13,384,128]{2,1,0:T(8,128)(2,1)}, u32[]{:S(2)}, u32[]{:S(2)}) collective-permute-start(bf16[13,384,128]{2,1,0:T(8,128)(2,1)} %fusion.65), channel_id=1, source_target_pairs={{1,3},{3,5},{5,7},{7,6},{6,4},{4,2},{2,0},{0,1},{9,11},{11,13},{13... | collective-permute-start | bytes 3833864 | tf_op jit(solution)/shard_map/ppermute | solution.py:224
  1098.9 78.0 %copy-start.37 = (bf16[1,512,768]{2,1,0:T(8,128)(2,1)S(1)}, bf16[1,512,768]{2,1,0:T(8,128)(2,1)}, u32[]{:S(2)}) copy-start(bf16[1,512,768]{2,1,0:T(8,128)(2,1)} %param.30) | copy-start | bytes 2359300
  1098.9 78.0 %copy-start.97 = (f32[768]{0:T(1024)S(1)}, f32[768]{0:T(1024)}, u32[]{:S(2)}) copy-start(f32[768]{0:T(1024)} %param.40) | copy-start | bytes 9220
  1098.9 78.0 %copy-start.99 = (f32[512]{0:T(512)S(1)}, f32[512]{0:T(512)}, u32[]{:S(2)}) copy-start(f32[512]{0:T(512)} %copy-done.98) | copy-start | bytes 6148
  1183.7 323.3 %all-reduce.16.cloned.1.call-start = ((), (), s32[]{:S(2)}) async-start(), calls=%async_computation.18 | async-start | bytes 3145728 | tf_op jit(solution)/shard_map/psum | solution.py:544
  1186.1 29.7 %collective-permute-start.23 = (bf16[13,384,128]{2,1,0:T(8,128)(2,1)S(1)}, bf16[13,384,128]{2,1,0:T(8,128)(2,1)S(1)}, u32[]{:S(2)}, u32[]{:S(2)}) collective-permute-start(bf16[13,384,128]{2,1,0:T(8,128)(2,1)S(1)} %fusion.58), channel_id=1, source_target_pairs={{3,1},{5,3},{7,5},{6,7},{4,6},{2,4},{0,2},{1,0},{11,9},{13,11},{15... | collective-permute-start | bytes 3833864 | tf_op jit(solution)/shard_map/ppermute | solution.py:227
  1189.4 29.4 %collective-permute-start.16 = (bf16[13,384,128]{2,1,0:T(8,128)(2,1)S(1)}, bf16[13,384,128]{2,1,0:T(8,128)(2,1)S(1)}, u32[]{:S(2)}, u32[]{:S(2)}) collective-permute-start(bf16[13,384,128]{2,1,0:T(8,128)(2,1)S(1)} %fusion.64), channel_id=1, source_target_pairs={{1,3},{3,5},{5,7},{7,6},{6,4},{4,2},{2,0},{0,1},{9,11},{11,13},{13... | collective-permute-start | bytes 3833864 | tf_op jit(solution)/shard_map/ppermute | solution.py:224
  1216.2 28.9 %collective-permute-start.24 = (bf16[13,384,128]{2,1,0:T(8,128)(2,1)S(1)}, bf16[13,384,128]{2,1,0:T(8,128)(2,1)S(1)}, u32[]{:S(2)}, u32[]{:S(2)}) collective-permute-start(bf16[13,384,128]{2,1,0:T(8,128)(2,1)S(1)} %fusion.57), channel_id=1, source_target_pairs={{3,1},{5,3},{7,5},{6,7},{4,6},{2,4},{0,2},{1,0},{11,9},{13,11},{15... | collective-permute-start | bytes 3833864 | tf_op jit(solution)/shard_map/ppermute | solution.py:227
  1219.2 28.6 %collective-permute-start.17 = (bf16[13,384,128]{2,1,0:T(8,128)(2,1)S(1)}, bf16[13,384,128]{2,1,0:T(8,128)(2,1)S(1)}, u32[]{:S(2)}, u32[]{:S(2)}) collective-permute-start(bf16[13,384,128]{2,1,0:T(8,128)(2,1)S(1)} %fusion.63), channel_id=1, source_target_pairs={{1,3},{3,5},{5,7},{7,6},{6,4},{4,2},{2,0},{0,1},{9,11},{11,13},{13... | collective-permute-start | bytes 3833864 | tf_op jit(solution)/shard_map/ppermute | solution.py:224
  1245.5 28.0 %collective-permute-start.25 = (bf16[13,384,128]{2,1,0:T(8,128)(2,1)S(1)}, bf16[13,384,128]{2,1,0:T(8,128)(2,1)S(1)}, u32[]{:S(2)}, u32[]{:S(2)}) collective-permute-start(bf16[13,384,128]{2,1,0:T(8,128)(2,1)S(1)} %fusion.56), channel_id=1, source_target_pairs={{3,1},{5,3},{7,5},{6,7},{4,6},{2,4},{0,2},{1,0},{11,9},{13,11},{15... | collective-permute-start | bytes 3833864 | tf_op jit(solution)/shard_map/ppermute | solution.py:227
  1248.2 28.2 %collective-permute-start.18 = (bf16[13,384,128]{2,1,0:T(8,128)(2,1)S(1)}, bf16[13,384,128]{2,1,0:T(8,128)(2,1)S(1)}, u32[]{:S(2)}, u32[]{:S(2)}) collective-permute-start(bf16[13,384,128]{2,1,0:T(8,128)(2,1)S(1)} %fusion.62), channel_id=1, source_target_pairs={{1,3},{3,5},{5,7},{7,6},{6,4},{4,2},{2,0},{0,1},{9,11},{11,13},{13... | collective-permute-start | bytes 3833864 | tf_op jit(solution)/shard_map/ppermute | solution.py:224
  1275.0 27.5 %collective-permute-start.26 = (bf16[13,384,128]{2,1,0:T(8,128)(2,1)}, bf16[13,384,128]{2,1,0:T(8,128)(2,1)}, u32[]{:S(2)}, u32[]{:S(2)}) collective-permute-start(bf16[13,384,128]{2,1,0:T(8,128)(2,1)} %fusion.55), channel_id=1, source_target_pairs={{3,1},{5,3},{7,5},{6,7},{4,6},{2,4},{0,2},{1,0},{11,9},{13,11},{15... | collective-permute-start | bytes 3833864 | tf_op jit(solution)/shard_map/ppermute | solution.py:227
  1278.0 28.8 %collective-permute-start.19 = (bf16[13,384,128]{2,1,0:T(8,128)(2,1)}, bf16[13,384,128]{2,1,0:T(8,128)(2,1)}, u32[]{:S(2)}, u32[]{:S(2)}) collective-permute-start(bf16[13,384,128]{2,1,0:T(8,128)(2,1)} %fusion.61), channel_id=1, source_target_pairs={{1,3},{3,5},{5,7},{7,6},{6,4},{4,2},{2,0},{0,1},{9,11},{11,13},{13... | collective-permute-start | bytes 3833864 | tf_op jit(solution)/shard_map/ppermute | solution.py:224
  1305.3 26.7 %collective-permute-start.27 = (bf16[13,384,128]{2,1,0:T(8,128)(2,1)}, bf16[13,384,128]{2,1,0:T(8,128)(2,1)}, u32[]{:S(2)}, u32[]{:S(2)}) collective-permute-start(bf16[13,384,128]{2,1,0:T(8,128)(2,1)} %fusion.54), channel_id=1, source_target_pairs={{3,1},{5,3},{7,5},{6,7},{4,6},{2,4},{0,2},{1,0},{11,9},{13,11},{15... | collective-permute-start | bytes 3833864 | tf_op jit(solution)/shard_map/ppermute | solution.py:227
  1309.6 26.6 %collective-permute-start.20 = (bf16[13,384,128]{2,1,0:T(8,128)(2,1)}, bf16[13,384,128]{2,1,0:T(8,128)(2,1)}, u32[]{:S(2)}, u32[]{:S(2)}) collective-permute-start(bf16[13,384,128]{2,1,0:T(8,128)(2,1)} %fusion.60), channel_id=1, source_target_pairs={{1,3},{3,5},{5,7},{7,6},{6,4},{4,2},{2,0},{0,1},{9,11},{11,13},{13... | collective-permute-start | bytes 3833864 | tf_op jit(solution)/shard_map/ppermute | solution.py:224
  (111 other events, 1784.9 us)
Sparse Core Ops, SparseCore 0:
  13.7 68.3 reduce-scatter.7
  85.6 63.6 all-gather.6
  150.9 26.8 all-gather.14
  182.0 26.9 all-gather.8
  276.3 26.9 all-gather.10
  410.9 62.6 all-gather.12
  663.6 36.5 reduce-scatter.9
  707.6 20.3 reduce-scatter.11
  760.4 36.4 reduce-scatter.13
  885.2 210.3 reduce-scatter.15
  1098.7 78.0 reduce-scatter.17
  1183.8 93.9 reduce-scatter.19
  1417.0 89.9 all-reduce.15
